TPU v7x, 128 devices: a whole 4x4x4 slice. The times are simulated.
128 devices in a mesh: dp: 8 (over x_hi, z), lm: 16 (over y, x_lo, core).
Axes of the slice: x: 4 (x_hi: 2, x_lo: 2; x = x_hi * 2 + x_lo), y: 4, z: 4, core: 2. Of those that a mesh axis runs over, the one named last changes fastest.
Arguments:
- queries: bfloat16 [16384, 256], P('dp', 'lm'), may hold values from -6 to 6
- landmarks: bfloat16 [65536, 256], P('lm'), may hold values from -6 to 6
- targets: bfloat16 [16384, 64], P('dp'), may hold values from -6 to 6
- ridge: float32 [64], replicated, may hold values from 4 to 64
Outputs:
- fit: float32 [16384, 64], P('dp')
All inputs are finite; a program needn't handle non-finite values.
Results may differ from a plain program's by a relative error of at most 0.0006.
The roundings to bfloat16 on the way count: a program that leaves them out, or rounds other values in their place, can miss the bound.
Values may be sent and summed in bfloat16 or wider, within the bound.
No kernel may reach another device: no remote copies, remote signals or barrier semaphores. Data moves between devices by JAX's collectives and lax.ppermute only.
A program may use at most 128 MiB of HBM per device.

v0:
```python
import jax
import jax.numpy as jnp
from jax import lax
from jax.sharding import PartitionSpec as P

ITERS = 2


sharpness = 8.0
epsilon = 1e-06


def normalize(rows):
    values = rows.astype(jnp.float32)
    scale = lax.rsqrt(jnp.sum(values * values, axis=1, keepdims=True) + epsilon)
    return (values * scale).astype(jnp.bfloat16)


def shards(queries, landmarks, targets, ridge):
    qhat = normalize(lax.all_gather(queries, "lm", axis=1, tiled=True))
    chat = normalize(landmarks)
    rows_dev = qhat.shape[0]
    lm_rows = chat.shape[0]
    width = qhat.shape[1]
    block_rows = min(512, rows_dev)
    total_rows = float(rows_dev * lax.axis_size("dp"))

    def tile_rows(block):
        scores = jnp.dot(block, chat.T, preferred_element_type=jnp.float32)
        tile = jnp.exp(2.0 * sharpness * scores).astype(jnp.bfloat16)
        values = tile.astype(jnp.float32)
        return (tile, jnp.sum(values * values, axis=0))

    tiles, column_sq = lax.map(tile_rows, qhat.reshape(rows_dev // block_rows, block_rows, width))
    kernel = tiles.reshape(rows_dev, lm_rows)
    rhs_part = lax.dot_general(
        kernel, targets, (((0,), (0,)), ((), ())), preferred_element_type=jnp.float32
    )
    rhs_sum, sq_sum = lax.psum((rhs_part, jnp.sum(column_sq, axis=0)), "dp")
    rhs = rhs_sum / total_rows
    precond = sq_sum[:, None] / total_rows + ridge[None, :]
    coefficients = jnp.zeros_like(rhs)
    residual = rhs
    direction = residual / precond
    norm_now = lax.psum(jnp.sum(residual * direction, axis=0), "lm")
    for step in range(ITERS):
        rounded = direction.astype(jnp.bfloat16)
        query_image = lax.psum(jnp.dot(kernel, rounded, preferred_element_type=jnp.float32), "lm")
        back_part = lax.dot_general(
            kernel,
            query_image.astype(jnp.bfloat16),
            (((0,), (0,)), ((), ())),
            preferred_element_type=jnp.float32,
        )
        back = lax.psum(back_part, "dp")
        image = back / total_rows + ridge[None, :] * direction
        alpha = norm_now / lax.psum(jnp.sum(direction * image, axis=0), "lm")
        coefficients = coefficients + alpha[None, :] * direction
        residual = residual - alpha[None, :] * image
        if step + 1 < ITERS:
            scaled = residual / precond
            norm_next = lax.psum(jnp.sum(residual * scaled, axis=0), "lm")
            direction = scaled + (norm_next / norm_now)[None, :] * direction
            norm_now = norm_next
    rounded_coef = coefficients.astype(jnp.bfloat16)
    return lax.psum(jnp.dot(kernel, rounded_coef, preferred_element_type=jnp.float32), "lm")


def solution(mesh):
    return jax.shard_map(
        shards,
        mesh=mesh,
        in_specs=(P("dp", "lm"), P("lm", None), P("dp", None), P()),
        out_specs=P("dp", None),
        check_vma=False,
    )
```

profile of v0, /device:TPU:1, one launch (start us, length us, event | category | flops | bytes accessed | tf_op | source)
XLA Modules:
  0.0 728.6 jit_solution(9330643112373927660)
XLA Ops:
  7.3 2.2 fusion.3
  9.6 1.9 fusion.4
  11.5 33.4 %all-gather.2.cloned.1.call-done = bf16[2048,256]{0,1:T(8,128)(2,1)} async-done(((bf16[2048,16]{0,1:T(8,128)(2,1)}), bf16[2048,256]{0,1:T(8,128)(2,1)}) %all-gather.2.cloned.1.call-update) | async-done | bytes 1048592 | tf_op jit(solution)/shard_map/all_gather | solution.py:20
  49.1 21.6 %while.12 = (s32[]{:T(128)}, bf16[4,512,4096]{2,1,0:T(8,128)(2,1)}, f32[4,4096]{1,0:T(4,128)S(1)}, bf16[4,512,256]{2,1,0:T(8,128)(2,1)}, bf16[4096,256]{1,0:T(8,128)(2,1)S(1)}, /*index=5*/s32[]{:T(128)}, s32[]{:T(128)}) while((s32[]{:T(128)}, bf16[4,512,4096]{2,1,0:T(8,128)(2,1)}, f32[4,4096]{1,0:T(4,128)S(1)}, ...), condition=%wide.region_4.5_spmd, body=%wide.region_2.4_spmd.sunk | while | flops 1084223488 | bytes 14992465 | solution.py:34
  49.1 4.2 bitcast_dynamic-update-slice_fusion.2
  54.5 4.2 bitcast_dynamic-update-slice_fusion.2
  59.9 4.3 bitcast_dynamic-update-slice_fusion.2
  65.3 4.2 bitcast_dynamic-update-slice_fusion.2
  70.7 9.8 %fusion.18 = f32[4096,64]{0,1:T(8,128)} fusion(bf16[2048,64]{0,1:T(8,128)(2,1)S(1)} %copy-done, bf16[2048,4096]{1,0:T(8,128)(2,1)} %bitcast.28), kind=kOutput, calls=%fused_computation.38 | convolution fusion | flops 1073741824 | bytes 18087936 | tf_op jit(solution)/shard_map/dot_general | solution.py:36
  80.6 35.1 %psum.78 = f32[4096]{0:T(1024)S(1)} all-reduce(f32[4096]{0:T(1024)S(1)} %reduce_sum.74), channel_id=1, replica_groups=mesh['dp'=8,'lm'=16] {'dp'}, use_global_device_ids=true, to_apply=%region_7.8 | all-reduce | flops 4096 | bytes 32768 | tf_op jit(solution)/shard_map/psum | solution.py:39
  115.7 46.8 %all-reduce.8.cloned.1.call-done = f32[4096,64]{0,1:T(8,128)} async-done(((f32[4096,64]{0,1:T(8,128)}), f32[4096,64]{0,1:T(8,128)}) %all-reduce.8.cloned.1.call-update) | async-done | bytes 1048592 | tf_op jit(solution)/shard_map/psum | solution.py:39
  162.5 8.5 %fusion.16 = f32[2048,64]{1,0:T(8,128)S(1)} fusion(bf16[2048,4096]{1,0:T(8,128)(2,1)} %bitcast.29, f32[4096,64]{0,1:T(8,128)} %all-reduce.8.cloned.1.call-done, f32[64]{0:T(128)S(1)} %copy-done.2, f32[4096]{0:T(1024)S(1)} %broadcast_multiply_fusion), kind=kOutput, calls=%fused_computation.33 | convolution fusion | flops 1074790400 | bytes 18366720 | tf_op jit(solution)/shard_map/dot_general | solution.py:48
  171.0 67.6 %all-reduce.15 = bf16[2048,64]{1,0:T(8,128)(2,1)S(1)} all-reduce(f32[2048,64]{1,0:T(8,128)S(1)} %fusion.16), channel_id=1, replica_groups=mesh['dp'=8,'lm'=16] {'lm'}, use_global_device_ids=true, to_apply=%region_10.11 | all-reduce | flops 131072 | bytes 786432 | tf_op jit(solution)/shard_map/psum | solution.py:48
  238.6 9.9 %fusion.20 = f32[4096,64]{0,1:T(8,128)} fusion(bf16[2048,4096]{1,0:T(8,128)(2,1)} %bitcast.30, bf16[2048,64]{1,0:T(8,128)(2,1)S(1)} %all-reduce.15), kind=kOutput, calls=%fused_computation.40 | convolution fusion | flops 1073741824 | bytes 18087936 | tf_op jit(solution)/shard_map/dot_general | solution.py:49
  248.8 81.9 %all-reduce.10.cloned.1.call-done = f32[4096,64]{0,1:T(8,128)} async-done(((f32[4096,64]{0,1:T(8,128)}), f32[4096,64]{0,1:T(8,128)}) %all-reduce.10.cloned.1.call-update) | async-done | bytes 1048592 | tf_op jit(solution)/shard_map/psum | solution.py:55
  332.5 32.9 %all-reduce = (f32[64]{0:T(128)S(1)}, f32[64]{0:T(128)S(1)}) all-reduce(f32[64]{0:T(128)S(1)} %get-tuple-element.36, f32[64]{0:T(128)S(1)} %get-tuple-element.35), channel_id=1, replica_groups=mesh['dp'=8,'lm'=16] {'lm'}, use_global_device_ids=true, to_apply=%region_9.10 | all-reduce | flops 128 | bytes 1024 | tf_op jit(solution)/shard_map/psum | solution.py:45
  367.3 27.2 %psum.83 = f32[64]{0:T(128)S(1)} all-reduce(f32[64]{0:T(128)S(1)} %multiply_reduce_fusion.2), channel_id=1, replica_groups=mesh['dp'=8,'lm'=16] {'lm'}, use_global_device_ids=true, to_apply=%region_15.16 | all-reduce | flops 64 | bytes 512 | tf_op jit(solution)/shard_map/psum | solution.py:62
  396.3 9.1 %fusion.11 = f32[2048,64]{1,0:T(8,128)} fusion(bf16[2048,4096]{1,0:T(8,128)(2,1)} %bitcast.31, f32[4096,64]{0,1:T(8,128)S(1)} %multiply_add_fusion), kind=kOutput, calls=%fused_computation.28 | convolution fusion | flops 1074003968 | bytes 18350080 | tf_op jit(solution)/shard_map/dot_general | solution.py:48
  405.4 62.5 %all-reduce.16 = bf16[2048,64]{1,0:T(8,128)(2,1)S(1)} all-reduce(f32[2048,64]{1,0:T(8,128)} %fusion.11), channel_id=1, replica_groups=mesh['dp'=8,'lm'=16] {'lm'}, use_global_device_ids=true, to_apply=%region_16.17 | all-reduce | flops 131072 | bytes 786432 | tf_op jit(solution)/shard_map/psum | solution.py:48
  467.9 9.9 %fusion.19 = f32[4096,64]{0,1:T(8,128)} fusion(bf16[2048,4096]{1,0:T(8,128)(2,1)} %bitcast.32, bf16[2048,64]{1,0:T(8,128)(2,1)S(1)} %all-reduce.16), kind=kOutput, calls=%fused_computation.39 | convolution fusion | flops 1073741824 | bytes 18087936 | tf_op jit(solution)/shard_map/dot_general | solution.py:49
  477.9 81.9 %all-reduce.12.cloned.1.call-done = f32[4096,64]{0,1:T(8,128)} async-done(((f32[4096,64]{0,1:T(8,128)}), f32[4096,64]{0,1:T(8,128)}) %all-reduce.12.cloned.1.call-update) | async-done | bytes 1048592 | tf_op jit(solution)/shard_map/psum | solution.py:55
  561.3 32.9 %psum.86 = f32[64]{0:T(128)S(1)} all-reduce(f32[64]{0:T(128)S(1)} %multiply_reduce_fusion.1), channel_id=1, replica_groups=mesh['dp'=8,'lm'=16] {'lm'}, use_global_device_ids=true, to_apply=%region_19.20 | all-reduce | flops 64 | bytes 512 | tf_op jit(solution)/shard_map/psum | solution.py:57
  594.2 11.8 %fusion.7 = f32[2048,64]{0,1:T(8,128)} fusion(bf16[2048,4096]{1,0:T(8,128)(2,1)} %bitcast.33, f32[4096,64]{0,1:T(8,128)S(1)} %multiply_add_fusion, f32[64]{0:T(128)S(1)} %div.39, f32[64]{0:T(128)S(1)} %div.35, f32[4096,64]{0,1:T(8,128)S(1)} %copy-done.1, f32[64]{0:T(128)S(1)} %copy-done.2, f32[4096]{0:T(1024)S(1)} %broadcast_multiply_fusion), kind=kOutput, calls=%fused_computation.24 | convolution fusion | flops 1075576832 | bytes 19415808 | tf_op jit(solution)/shard_map/dot_general | solution.py:66
  606.1 114.2 %all-reduce.14.cloned.1.call-done = f32[2048,64]{0,1:T(8,128)} async-done(((f32[2048,64]{0,1:T(8,128)}), f32[2048,64]{0,1:T(8,128)}) %all-reduce.14.cloned.1.call-update) | async-done | bytes 524304 | tf_op jit(solution)/shard_map/psum | solution.py:66
  (41 shorter events, 18.8 us)
Async XLA Ops:
  6.5 64.1 %copy-start = (bf16[2048,64]{0,1:T(8,128)(2,1)S(1)}, bf16[2048,64]{0,1:T(8,128)(2,1)}, u32[]{:S(2)}) copy-start(bf16[2048,64]{0,1:T(8,128)(2,1)} %param.8) | copy-start | bytes 786436
  6.5 38.3 %all-gather.2.cloned.1.call-start = ((), (), s32[]{:S(2)}) async-start(), calls=%async_computation | async-start | bytes 1114112 | tf_op jit(solution)/shard_map/all_gather | solution.py:20
  7.3 155.3 %all-reduce.8.cloned.1.call-start = ((), (), s32[]{:S(2)}) async-start(), calls=%async_computation.1 | async-start | bytes 2097152 | tf_op jit(solution)/shard_map/psum | solution.py:39
  70.7 91.9 %copy-start.2 = (f32[64]{0:T(128)S(1)}, f32[64]{0:T(128)}, u32[]{:S(2)}) copy-start(f32[64]{0:T(128)} %param.9) | copy-start | bytes 772
  80.5 250.2 %all-reduce.10.cloned.1.call-start = ((), (), s32[]{:S(2)}) async-start(), calls=%async_computation.2 | async-start | bytes 2097152 | tf_op jit(solution)/shard_map/psum | solution.py:55
  238.6 92.1 %copy-start.1 = (f32[4096,64]{0,1:T(8,128)S(1)}, f32[4096,64]{0,1:T(8,128)}, u32[]{:S(2)}) copy-start(f32[4096,64]{0,1:T(8,128)} %all-reduce.8.cloned.1.call-done) | copy-start | bytes 3145732
  248.6 311.1 %all-reduce.12.cloned.1.call-start = ((), (), s32[]{:S(2)}) async-start(), calls=%async_computation.3 | async-start | bytes 2097152 | tf_op jit(solution)/shard_map/psum | solution.py:55
  477.8 242.4 %all-reduce.14.cloned.1.call-start = ((), (), s32[]{:S(2)}) async-start(), calls=%async_computation.4 | async-start | bytes 1048576 | tf_op jit(solution)/shard_map/psum | solution.py:66
Sparse Core Ops, SparseCore 0:
  9.0 35.7 all-gather.1
  80.7 81.8 all-reduce.7
  248.7 81.9 all-reduce.9
  478.0 81.7 all-reduce.11
  606.2 113.9 all-reduce.13
where the time goes:
time: 729 us
  waiting for transfers between devices  359 us (49%)
  blocking collectives  258 us (35%)
  matrix products  76 us (10%)
  other arithmetic  17.6 us (2%)
  between operations  13.3 us (2%)
    psum x2, waiting for transfers between devices, shards(): back = lax.psum(back_part, 'dp')  164 us
    psum x2, blocking collectives, shards(): lax.psum(jnp.dot(kernel, rounded, preferred_element_type=jnp.float32), 'lm')  130 us
    psum x1, waiting for transfers between devices, shards(): lax.psum(jnp.dot(kernel, rounded_coef, preferred_element_type=jnp.float32...  114 us
    psum x1, waiting for transfers between devices, shards(): rhs_sum, sq_sum = lax.psum((rhs_part, jnp.sum(column_sq, axis=0)), 'dp')  46.8 us
    psum x1, blocking collectives, shards(): rhs_sum, sq_sum = lax.psum((rhs_part, jnp.sum(column_sq, axis=0)), 'dp')  35.1 us
    all_gather x1, waiting for transfers between devices, shards(): qhat = normalize(lax.all_gather(queries, 'lm', axis=1, tiled=True))  33.4 us
    psum x1, blocking collectives, shards(): norm_now = lax.psum(jnp.sum(residual * direction, axis=0), 'lm')  32.9 us
    psum x1, blocking collectives, shards(): alpha = norm_now / lax.psum(jnp.sum(direction * image, axis=0), 'lm')  32.9 us
  transfers between devices with their start and end apart: 5, of which 5 were waited for; matrix products, arithmetic and copies ran while one was open for 1% of the time, Pallas kernels for 0%

commit v1 on v0

v1 whole, which is shorter than its diff:
```python
import jax
import jax.numpy as jnp
from jax import lax
from jax.sharding import PartitionSpec as P

ITERS = 2


sharpness = 8.0
epsilon = 1e-06


def normalize(rows):
    values = rows.astype(jnp.float32)
    scale = lax.rsqrt(jnp.sum(values * values, axis=1, keepdims=True) + epsilon)
    return (values * scale).astype(jnp.bfloat16)


def _pairs(n, k):
    return [(i, i ^ k) for i in range(n)]


def _bits(n):
    bits = []
    k = 1
    while k < n:
        bits.append(k)
        k *= 2
    return bits


def tree_sum(x, axis):
    n = lax.axis_size(axis)
    for k in _bits(n):
        x = x + lax.ppermute(x, axis, _pairs(n, k))
    return x


def ring_sum(x, axis):
    n = lax.axis_size(axis)
    idx = lax.axis_index(axis)
    bits = _bits(n)
    for k in bits:
        half = x.shape[0] // 2
        upper = (idx // k) % 2 == 1
        lo, hi = x[:half], x[half:]
        keep = jnp.where(upper, hi, lo)
        send = jnp.where(upper, lo, hi)
        x = keep + lax.ppermute(send, axis, _pairs(n, k))
    for k in reversed(bits):
        upper = (idx // k) % 2 == 1
        other = lax.ppermute(x, axis, _pairs(n, k))
        x = jnp.where(upper, jnp.concatenate([other, x], 0), jnp.concatenate([x, other], 0))
    return x


def shards(queries, landmarks, targets, ridge):
    qhat = normalize(lax.all_gather(queries, "lm", axis=1, tiled=True))
    chat = normalize(landmarks)
    rows_dev = qhat.shape[0]
    lm_rows = chat.shape[0]
    width = qhat.shape[1]
    n_tg = targets.shape[1]
    block_rows = min(512, rows_dev)
    total_rows = float(rows_dev * lax.axis_size("dp"))
    first_dp = lax.axis_index("dp") == 0

    def tile_rows(block):
        scores = jnp.dot(block, chat.T, preferred_element_type=jnp.float32)
        tile = jnp.exp(2.0 * sharpness * scores).astype(jnp.bfloat16)
        values = tile.astype(jnp.float32)
        return (tile, jnp.sum(values * values, axis=0))

    tiles, column_sq = lax.map(tile_rows, qhat.reshape(rows_dev // block_rows, block_rows, width))
    kernel = tiles.reshape(rows_dev, lm_rows)
    rhs_part = lax.dot_general(
        kernel, targets, (((0,), (0,)), ((), ())), preferred_element_type=jnp.float32
    )
    stacked = ring_sum(jnp.concatenate([rhs_part, jnp.sum(column_sq, axis=0)[:, None]], 1), "dp")
    rhs = stacked[:, :n_tg] / total_rows
    precond = stacked[:, n_tg:] / total_rows + ridge[None, :]
    coefficients = jnp.zeros_like(rhs)
    residual = rhs
    direction = residual / precond
    norm_part = jnp.sum(residual * direction, axis=0)
    norm_now = None
    for step in range(ITERS):
        rounded = direction.astype(jnp.bfloat16)
        image_part = jnp.dot(kernel, rounded, preferred_element_type=jnp.float32)
        if norm_now is None:
            extra = jnp.zeros((rows_dev, 1), jnp.float32).at[:n_tg, 0].set(norm_part)
            summed = ring_sum(jnp.concatenate([image_part, extra], 1), "lm")
            query_image = summed[:, :n_tg]
            norm_now = summed[:n_tg, n_tg]
        else:
            query_image = ring_sum(image_part, "lm")
        back_part = lax.dot_general(
            kernel,
            query_image.astype(jnp.bfloat16),
            (((0,), (0,)), ((), ())),
            preferred_element_type=jnp.float32,
        )
        dot_part = jnp.sum(direction * back_part, axis=0) / total_rows + jnp.where(
            first_dp, ridge * jnp.sum(direction * direction, axis=0), 0.0
        )
        dot_all = tree_sum(tree_sum(dot_part, "dp"), "lm")
        back = ring_sum(back_part, "dp")
        image = back / total_rows + ridge[None, :] * direction
        alpha = norm_now / dot_all
        coefficients = coefficients + alpha[None, :] * direction
        residual = residual - alpha[None, :] * image
        if step + 1 < ITERS:
            scaled = residual / precond
            norm_next = tree_sum(jnp.sum(residual * scaled, axis=0), "lm")
            direction = scaled + (norm_next / norm_now)[None, :] * direction
            norm_now = norm_next
    rounded_coef = coefficients.astype(jnp.bfloat16)
    return ring_sum(jnp.dot(kernel, rounded_coef, preferred_element_type=jnp.float32), "lm")


def solution(mesh):
    return jax.shard_map(
        shards,
        mesh=mesh,
        in_specs=(P("dp", "lm"), P("lm", None), P("dp", None), P()),
        out_specs=P("dp", None),
        check_vma=False,
    )
```

time: 729 us -> 418 us (0.57)
  blocking collectives: 258 us -> 0 us
  waiting for transfers between devices: 359 us -> 204 us
  starting transfers between devices: 0.35 us -> 111 us
  matrix products: 76 us -> 65.3 us
    psum x4 -> x0, waiting for transfers between devices: 325 us -> none  [the longest x2 164 us: shards(): back = lax.psum(back_part, 'dp')]
    psum x6 -> x0, blocking collectives: 258 us -> none  [the longest x2 130 us: shards(): lax.psum(jnp.dot(kernel, rounded, preferred_element_type=jnp.float32), 'lm')]
    ppermute x0 -> x54, waiting for transfers between devices: none -> 170 us  [the longest x18 74.9 us: ring_sum(): x = keep + lax.ppermute(send, axis, _pairs(n, k))]
    ppermute x0 -> x54, starting transfers between devices: none -> 111 us  [the longest x18 42.8 us: ring_sum(): other = lax.ppermute(x, axis, _pairs(n, k))]
    dot_general x2, matrix products: 19.8 us -> 12.1 us  [shards(): lax.dot_general(kernel, query_image.astype(jnp.bfloat16), (((0,), (0,)),...]
  transfers between devices with their start and end apart: 5 -> 55, of which waited for: 5 -> 54; matrix products, arithmetic and copies ran while one was open for 1% -> 1% of each run, Pallas kernels for 0% -> 0%
where the time goes in v1:
time: 418 us; the launch traced here: 412 us
  waiting for transfers between devices  204 us (49%)
  starting transfers between devices  111 us (27%)
  matrix products  65.3 us (16%)
  other arithmetic  14.7 us (4%)
  between operations  14.3 us (3%)
    ppermute x18, waiting for transfers between devices, ring_sum(): x = keep + lax.ppermute(send, axis, _pairs(n, k))  74.9 us
    ppermute x18, waiting for transfers between devices, ring_sum(): other = lax.ppermute(x, axis, _pairs(n, k))  55.2 us
    ppermute x18, starting transfers between devices, ring_sum(): other = lax.ppermute(x, axis, _pairs(n, k))  42.8 us
    ppermute x18, waiting for transfers between devices, tree_sum(): x = x + lax.ppermute(x, axis, _pairs(n, k))  40 us
    ppermute x18, starting transfers between devices, ring_sum(): x = keep + lax.ppermute(send, axis, _pairs(n, k))  35.2 us
    all_gather x1, waiting for transfers between devices, shards(): qhat = normalize(lax.all_gather(queries, 'lm', axis=1, tiled=True))  33.4 us
    ppermute x18, starting transfers between devices, tree_sum(): x = x + lax.ppermute(x, axis, _pairs(n, k))  32.8 us
    dot_general x2, matrix products, shards(): image_part = jnp.dot(kernel, rounded, preferred_element_type=jnp.float32)  22.1 us
  transfers between devices with their start and end apart: 55, of which 54 were waited for; matrix products, arithmetic and copies ran while one was open for 1% of the time, Pallas kernels for 0%

profile of v1, /device:TPU:1, one launch (start us, length us, event | category | flops | bytes accessed | tf_op | source)
XLA Modules:
  0.0 411.9 jit_solution(17127665462556096787)
XLA Ops:
  11.5 33.4 %all-gather.2.cloned.1.call-done = bf16[2048,256]{0,1:T(8,128)(2,1)} async-done(((bf16[2048,16]{0,1:T(8,128)(2,1)}), bf16[2048,256]{0,1:T(8,128)(2,1)}) %all-gather.2.cloned.1.call-update) | async-done | bytes 1048592 | tf_op jit(solution)/shard_map/all_gather | solution.py:58
  49.1 21.7 %while.13 = (s32[]{:T(128)}, bf16[4,512,4096]{2,1,0:T(8,128)(2,1)}, f32[4,4096]{1,0:T(4,128)S(1)}, bf16[4,512,256]{2,1,0:T(8,128)(2,1)}, bf16[4096,256]{1,0:T(8,128)(2,1)S(1)}, /*index=5*/s32[]{:T(128)}, s32[]{:T(128)}) while((s32[]{:T(128)}, bf16[4,512,4096]{2,1,0:T(8,128)(2,1)}, f32[4,4096]{1,0:T(4,128)S(1)}, ...), condition=%wide.region_4.5_spmd, body=%wide.region_2.4_spmd.sunk | while | flops 1084223488 | bytes 14992473 | solution.py:74
  49.1 4.2 %bitcast_dynamic-update-slice_fusion.2 = (bf16[4,512,4096]{2,1,0:T(8,128)(2,1)}, bf16[512,4096]{1,0:T(8,128)(2,1)S(1)}) fusion(bf16[4,512,4096]{2,1,0:T(8,128)(2,1)} %get-tuple-element.111, s32[]{:T(128)S(6)} %copy.11, bf16[4096,256]{1,0:T(8,128)(2,1)S(1)} %get-tuple-element.121, bf16[4,512,256]{2,1,0:T(8,128)(2,1)} %get-tuple-element.120), kind=kOutput, calls=%fused_computation.2.clone.1 | convolution fusion | flops 1077936128 | bytes 10748928 | tf_op jit(solution)/shard_map/while/body/eval_jaxpr/dot_general | solution.py:69
  54.5 4.3 %bitcast_dynamic-update-slice_fusion.2 = (bf16[4,512,4096]{2,1,0:T(8,128)(2,1)}, bf16[512,4096]{1,0:T(8,128)(2,1)S(1)}) fusion(bf16[4,512,4096]{2,1,0:T(8,128)(2,1)} %get-tuple-element.111, s32[]{:T(128)S(6)} %copy.11, bf16[4096,256]{1,0:T(8,128)(2,1)S(1)} %get-tuple-element.121, bf16[4,512,256]{2,1,0:T(8,128)(2,1)} %get-tuple-element.120), kind=kOutput, calls=%fused_computation.2.clone.1 | convolution fusion | flops 1077936128 | bytes 10748928 | tf_op jit(solution)/shard_map/while/body/eval_jaxpr/dot_general | solution.py:69
  60.0 4.3 %bitcast_dynamic-update-slice_fusion.2 = (bf16[4,512,4096]{2,1,0:T(8,128)(2,1)}, bf16[512,4096]{1,0:T(8,128)(2,1)S(1)}) fusion(bf16[4,512,4096]{2,1,0:T(8,128)(2,1)} %get-tuple-element.111, s32[]{:T(128)S(6)} %copy.11, bf16[4096,256]{1,0:T(8,128)(2,1)S(1)} %get-tuple-element.121, bf16[4,512,256]{2,1,0:T(8,128)(2,1)} %get-tuple-element.120), kind=kOutput, calls=%fused_computation.2.clone.1 | convolution fusion | flops 1077936128 | bytes 10748928 | tf_op jit(solution)/shard_map/while/body/eval_jaxpr/dot_general | solution.py:69
  65.5 4.2 %bitcast_dynamic-update-slice_fusion.2 = (bf16[4,512,4096]{2,1,0:T(8,128)(2,1)}, bf16[512,4096]{1,0:T(8,128)(2,1)S(1)}) fusion(bf16[4,512,4096]{2,1,0:T(8,128)(2,1)} %get-tuple-element.111, s32[]{:T(128)S(6)} %copy.11, bf16[4096,256]{1,0:T(8,128)(2,1)S(1)} %get-tuple-element.121, bf16[4,512,256]{2,1,0:T(8,128)(2,1)} %get-tuple-element.120), kind=kOutput, calls=%fused_computation.2.clone.1 | convolution fusion | flops 1077936128 | bytes 10748928 | tf_op jit(solution)/shard_map/while/body/eval_jaxpr/dot_general | solution.py:69
  70.9 8.8 %fusion.29 = f32[4096,64]{0,1:T(8,128)S(1)} fusion(bf16[2048,64]{0,1:T(8,128)(2,1)S(1)} %copy-done, bf16[2048,4096]{1,0:T(8,128)(2,1)} %bitcast.35), kind=kOutput, calls=%fused_computation.113 | convolution fusion | flops 1073741824 | bytes 18087936 | tf_op jit(solution)/shard_map/dot_general | solution.py:76
  81.1 13.3 %collective-permute-done = f32[2048,65]{0,1:T(8,128)S(1)} collective-permute-done((f32[2048,65]{0,1:T(8,128)S(1)}, f32[2048,65]{0,1:T(8,128)S(1)}, u32[]{:S(2)}, u32[]{:S(2)}) %collective-permute-start) | collective-permute-done | bytes 532512 | tf_op jit(solution)/shard_map/ppermute | solution.py:49
  97.5 6.0 %collective-permute-done.1 = f32[1024,65]{0,1:T(8,128)S(1)} collective-permute-done((f32[1024,65]{0,1:T(8,128)S(1)}, f32[1024,65]{0,1:T(8,128)S(1)}, u32[]{:S(2)}, u32[]{:S(2)}) %collective-permute-start.1) | collective-permute-done | bytes 266272 | tf_op jit(solution)/shard_map/ppermute | solution.py:49
  123.6 11.5 %collective-permute-done.5 = f32[2048,65]{0,1:T(8,128)S(1)} collective-permute-done((f32[2048,65]{0,1:T(8,128)S(1)}, f32[2048,65]{0,1:T(8,128)S(1)}, u32[]{:S(2)}, u32[]{:S(2)}) %collective-permute-start.5) | collective-permute-done | bytes 532512 | tf_op jit(solution)/shard_map/ppermute | solution.py:52
  135.6 11.0 %fusion.19 = f32[2048,64]{0,1:T(8,128)S(1)} fusion(bf16[2048,4096]{1,0:T(8,128)(2,1)} %bitcast.36, f32[4096,65]{0,1:T(8,128)S(1)} %maximum_select_fusion, f32[64]{0:T(128)S(1)} %copy-done.1, f32[4096]{0:T(1024)S(1)} %bitcast.46), kind=kOutput, calls=%fused_computation.52 | convolution fusion | flops 1074790400 | bytes 18366976 | tf_op jit(solution)/shard_map/dot_general | solution.py:89
  146.7 5.4 %collective-permute-start.6 = (f32[1024,65]{0,1:T(8,128)S(1)}, f32[1024,65]{0,1:T(8,128)S(1)}, u32[]{:S(2)}, u32[]{:S(2)}) collective-permute-start(f32[1024,65]{0,1:T(8,128)S(1)} %slice_select_fusion.1), channel_id=1, source_target_pairs={{0,1},{1,0},{2,3},{3,2},{4,5},{5,4},{6,7},{7,6},{8,9},{9,8},{10,11... | collective-permute-start | bytes 798728 | tf_op jit(solution)/shard_map/ppermute | solution.py:49
  154.3 4.2 %collective-permute-done.7 = f32[512,65]{0,1:T(8,128)S(1)} collective-permute-done((f32[512,65]{0,1:T(8,128)S(1)}, f32[512,65]{0,1:T(8,128)S(1)}, u32[]{:S(2)}, u32[]{:S(2)}) %collective-permute-start.7) | collective-permute-done | bytes 133152 | tf_op jit(solution)/shard_map/ppermute | solution.py:49
  179.1 6.4 %collective-permute-start.13 = (f32[1024,65]{0,1:T(8,128)S(1)}, f32[1024,65]{0,1:T(8,128)S(1)}, u32[]{:S(2)}, u32[]{:S(2)}) collective-permute-start(f32[1024,65]{0,1:T(8,128)S(1)} %maximum_select_fusion.8), channel_id=1, source_target_pairs={{0,1},{1,0},{2,3},{3,2},{4,5},{5,4},{6,7},{7,6},{8,9},{9,8},{10,11... | collective-permute-start | bytes 798728 | tf_op jit(solution)/shard_map/ppermute | solution.py:52
  186.8 9.0 %multiply_reduce_fusion.4 = (f32[64]{0:T(128)S(1)}, f32[64]{0:T(128)S(1)}, f32[4096,64]{0,1:T(8,128)S(1)}) fusion(f32[64]{0:T(128)S(1)} %copy-done.1, f32[4096]{0:T(1024)S(1)} %bitcast.47, f32[4096,65]{0,1:T(8,128)S(1)} %maximum_select_fusion, bf16[2048,4096]{1,0:T(8,128)(2,1)} %bitcast.37, f32[2048,65]{0,1:T(8,128)S(1)} %maximum_select_fusion.3), kind=kOutput, calls=%fused_computation.32 | convolution fusion | flops 1075576832 | bytes 19153920 | tf_op jit(solution)/shard_map/dot_general | solution.py:97
  197.0 12.0 %collective-permute-done.21 = f32[2048,64]{0,1:T(8,128)S(1)} collective-permute-done((f32[2048,64]{0,1:T(8,128)S(1)}, f32[2048,64]{0,1:T(8,128)S(1)}, u32[]{:S(2)}, u32[]{:S(2)}) %collective-permute-start.21) | collective-permute-done | bytes 524320 | tf_op jit(solution)/shard_map/ppermute | solution.py:49
  211.6 5.8 %collective-permute-done.22 = f32[1024,64]{0,1:T(8,128)S(1)} collective-permute-done((f32[1024,64]{0,1:T(8,128)S(1)}, f32[1024,64]{0,1:T(8,128)S(1)}, u32[]{:S(2)}, u32[]{:S(2)}) %collective-permute-start.22) | collective-permute-done | bytes 262176 | tf_op jit(solution)/shard_map/ppermute | solution.py:49
  230.7 4.3 %collective-permute-done.25 = f32[1024,64]{0,1:T(8,128)S(1)} collective-permute-done((f32[1024,64]{0,1:T(8,128)S(1)}, f32[1024,64]{0,1:T(8,128)S(1)}, u32[]{:S(2)}, u32[]{:S(2)}) %collective-permute-start.25) | collective-permute-done | bytes 262176 | tf_op jit(solution)/shard_map/ppermute | solution.py:52
  236.7 9.8 %collective-permute-done.14 = f32[64]{0:T(128)S(1)} collective-permute-done((f32[64]{0:T(128)S(1)}, f32[64]{0:T(128)S(1)}, u32[]{:S(2)}, u32[]{:S(2)}) %collective-permute-start.14) | collective-permute-done | bytes 288 | tf_op jit(solution)/shard_map/ppermute | solution.py:35
  254.4 7.8 %collective-permute-start.17 = (f32[64]{0:T(128)S(1)}, f32[64]{0:T(128)S(1)}, u32[]{:S(2)}, u32[]{:S(2)}) collective-permute-start(f32[64]{0:T(128)S(1)} %add.250), channel_id=1, source_target_pairs={{0,1},{1,0},{2,3},{3,2},{4,5},{5,4},{6,7},{7,6},{8,9},{9,8},{10,11... | collective-permute-start | bytes 776 | tf_op jit(solution)/shard_map/ppermute | solution.py:35
  286.5 11.1 %fusion.16 = f32[2048,64]{0,1:T(8,128)S(1)} fusion(bf16[2048,4096]{1,0:T(8,128)(2,1)} %bitcast.38, f32[4096,64]{0,1:T(8,128)S(1)} %get-tuple-element.60), kind=kOutput, calls=%fused_computation.48 | convolution fusion | flops 1074003968 | bytes 18350080 | tf_op jit(solution)/shard_map/dot_general | solution.py:89
  325.4 7.2 %collective-permute-start.38 = (bf16[1024,64]{0,1:T(8,128)(2,1)S(1)}, bf16[1024,64]{0,1:T(8,128)(2,1)S(1)}, u32[]{:S(2)}, u32[]{:S(2)}) collective-permute-start(bf16[1024,64]{0,1:T(8,128)(2,1)S(1)} %maximum_select_fusion.10), channel_id=1, source_target_pairs={{0,1},{1,0},{2,3},{3,2},{4,5},{5,4},{6,7},{7,6},{8,9},{9,8},{10,11... | collective-permute-start | bytes 393224 | tf_op jit(solution)/shard_map/ppermute | solution.py:52
  360.9 5.3 %fusion.13 = f32[2048,64]{0,1:T(8,128)S(1)} fusion(bf16[2048,4096]{1,0:T(8,128)(2,1)S(1)} %bitcast.42, f32[4096,64]{0,1:T(8,128)S(1)} %get-tuple-element.60, f32[64]{0:T(128)S(1)} %add_divide_fusion.2, f32[64]{0:T(128)S(1)} %add_divide_fusion.3, f32[4096,65]{0,1:T(8,128)S(1)} %maximum_select_fusion, f32[64]{0:T(128)S(1)} %copy-done.1, f32[4096]{0:T(1024)S(1)} %bitcast.50), kind=kOutput, calls=%fused_computation.41 | convolution fusion | flops 1075576832 | bytes 19416576 | tf_op jit(solution)/shard_map/dot_general | solution.py:118
  395.8 6.8 %collective-permute-start.53 = (f32[1024,64]{0,1:T(8,128)S(1)}, f32[1024,64]{0,1:T(8,128)S(1)}, u32[]{:S(2)}, u32[]{:S(2)}) collective-permute-start(f32[1024,64]{0,1:T(8,128)S(1)} %maximum_select_fusion.11), channel_id=1, source_target_pairs={{0,1},{1,0},{2,3},{3,2},{4,5},{5,4},{6,7},{7,6},{8,9},{9,8},{10,11... | collective-permute-start | bytes 786440 | tf_op jit(solution)/shard_map/ppermute | solution.py:52
  (206 shorter events, 201.2 us)
Async XLA Ops:
  6.5 38.3 %all-gather.2.cloned.1.call-start = ((), (), s32[]{:S(2)}) async-start(), calls=%async_computation | async-start | bytes 1114112 | tf_op jit(solution)/shard_map/all_gather | solution.py:58
  79.7 14.7 %collective-permute-start = (f32[2048,65]{0,1:T(8,128)S(1)}, f32[2048,65]{0,1:T(8,128)S(1)}, u32[]{:S(2)}, u32[]{:S(2)}) collective-permute-start(f32[2048,65]{0,1:T(8,128)S(1)} %broadcast_select_fusion), channel_id=1, source_target_pairs={{0,16},{16,0},{32,48},{48,32},{64,80},{80,64},{96,112},{112,96},{1... | collective-permute-start | bytes 1597448 | tf_op jit(solution)/shard_map/ppermute | solution.py:49
  94.5 9.0 %collective-permute-start.1 = (f32[1024,65]{0,1:T(8,128)S(1)}, f32[1024,65]{0,1:T(8,128)S(1)}, u32[]{:S(2)}, u32[]{:S(2)}) collective-permute-start(f32[1024,65]{0,1:T(8,128)S(1)} %slice_select_fusion.2), channel_id=1, source_target_pairs={{0,32},{16,48},{32,0},{48,16},{64,96},{80,112},{96,64},{112,80},{1... | collective-permute-start | bytes 798728 | tf_op jit(solution)/shard_map/ppermute | solution.py:49
  103.6 5.6 %collective-permute-start.2 = (f32[512,65]{0,1:T(8,128)S(1)}, f32[512,65]{0,1:T(8,128)S(1)}, u32[]{:S(2)}, u32[]{:S(2)}) collective-permute-start(f32[512,65]{0,1:T(8,128)S(1)} %slice_select_fusion.7), channel_id=1, source_target_pairs={{0,64},{16,80},{32,96},{48,112},{64,0},{80,16},{96,32},{112,48},{1... | collective-permute-start | bytes 399368 | tf_op jit(solution)/shard_map/ppermute | solution.py:49
  109.2 5.6 %collective-permute-start.3 = (f32[512,65]{0,1:T(8,128)S(1)}, f32[512,65]{0,1:T(8,128)S(1)}, u32[]{:S(2)}, u32[]{:S(2)}) collective-permute-start(f32[512,65]{0,1:T(8,128)S(1)} %select_add_fusion.8), channel_id=1, source_target_pairs={{0,64},{16,80},{32,96},{48,112},{64,0},{80,16},{96,32},{112,48},{1... | collective-permute-start | bytes 399368 | tf_op jit(solution)/shard_map/ppermute | solution.py:52
  114.8 7.2 %collective-permute-start.4 = (f32[1024,65]{0,1:T(8,128)S(1)}, f32[1024,65]{0,1:T(8,128)S(1)}, u32[]{:S(2)}, u32[]{:S(2)}) collective-permute-start(f32[1024,65]{0,1:T(8,128)S(1)} %maximum_select_fusion.7), channel_id=1, source_target_pairs={{0,32},{16,48},{32,0},{48,16},{64,96},{80,112},{96,64},{112,80},{1... | collective-permute-start | bytes 798728 | tf_op jit(solution)/shard_map/ppermute | solution.py:52
  122.1 13.0 %collective-permute-start.5 = (f32[2048,65]{0,1:T(8,128)S(1)}, f32[2048,65]{0,1:T(8,128)S(1)}, u32[]{:S(2)}, u32[]{:S(2)}) collective-permute-start(f32[2048,65]{0,1:T(8,128)S(1)} %maximum_select_fusion.2), channel_id=1, source_target_pairs={{0,16},{16,0},{32,48},{48,32},{64,80},{80,64},{96,112},{112,96},{1... | collective-permute-start | bytes 1597448 | tf_op jit(solution)/shard_map/ppermute | solution.py:52
  146.7 6.6 %collective-permute-start.6 = (f32[1024,65]{0,1:T(8,128)S(1)}, f32[1024,65]{0,1:T(8,128)S(1)}, u32[]{:S(2)}, u32[]{:S(2)}) collective-permute-start(f32[1024,65]{0,1:T(8,128)S(1)} %slice_select_fusion.1), channel_id=1, source_target_pairs={{0,1},{1,0},{2,3},{3,2},{4,5},{5,4},{6,7},{7,6},{8,9},{9,8},{10,11... | collective-permute-start | bytes 798728 | tf_op jit(solution)/shard_map/ppermute | solution.py:49
  153.4 5.1 %collective-permute-start.7 = (f32[512,65]{0,1:T(8,128)S(1)}, f32[512,65]{0,1:T(8,128)S(1)}, u32[]{:S(2)}, u32[]{:S(2)}) collective-permute-start(f32[512,65]{0,1:T(8,128)S(1)} %slice_select_fusion.6), channel_id=1, source_target_pairs={{0,2},{1,3},{2,0},{3,1},{4,6},{5,7},{6,4},{7,5},{8,10},{9,11},{10,... | collective-permute-start | bytes 399368 | tf_op jit(solution)/shard_map/ppermute | solution.py:49
  179.1 7.6 %collective-permute-start.13 = (f32[1024,65]{0,1:T(8,128)S(1)}, f32[1024,65]{0,1:T(8,128)S(1)}, u32[]{:S(2)}, u32[]{:S(2)}) collective-permute-start(f32[1024,65]{0,1:T(8,128)S(1)} %maximum_select_fusion.8), channel_id=1, source_target_pairs={{0,1},{1,0},{2,3},{3,2},{4,5},{5,4},{6,7},{7,6},{8,9},{9,8},{10,11... | collective-permute-start | bytes 798728 | tf_op jit(solution)/shard_map/ppermute | solution.py:52
  195.8 13.2 %collective-permute-start.21 = (f32[2048,64]{0,1:T(8,128)S(1)}, f32[2048,64]{0,1:T(8,128)S(1)}, u32[]{:S(2)}, u32[]{:S(2)}) collective-permute-start(f32[2048,64]{0,1:T(8,128)S(1)} %slice_select_fusion), channel_id=1, source_target_pairs={{0,16},{16,0},{32,48},{48,32},{64,80},{80,64},{96,112},{112,96},{1... | collective-permute-start | bytes 1572872 | tf_op jit(solution)/shard_map/ppermute | solution.py:49
  209.1 8.2 %collective-permute-start.22 = (f32[1024,64]{0,1:T(8,128)S(1)}, f32[1024,64]{0,1:T(8,128)S(1)}, u32[]{:S(2)}, u32[]{:S(2)}) collective-permute-start(f32[1024,64]{0,1:T(8,128)S(1)} %slice_select_fusion.5), channel_id=1, source_target_pairs={{0,32},{16,48},{32,0},{48,16},{64,96},{80,112},{96,64},{112,80},{1... | collective-permute-start | bytes 786440 | tf_op jit(solution)/shard_map/ppermute | solution.py:49
  217.4 5.4 %collective-permute-start.23 = (f32[512,64]{0,1:T(8,128)S(1)}, f32[512,64]{0,1:T(8,128)S(1)}, u32[]{:S(2)}, u32[]{:S(2)}) collective-permute-start(f32[512,64]{0,1:T(8,128)S(1)} %slice_select_fusion.10), channel_id=1, source_target_pairs={{0,64},{16,80},{32,96},{48,112},{64,0},{80,16},{96,32},{112,48},{1... | collective-permute-start | bytes 393224 | tf_op jit(solution)/shard_map/ppermute | solution.py:49
  222.8 5.4 %collective-permute-start.24 = (f32[512,64]{0,1:T(8,128)S(1)}, f32[512,64]{0,1:T(8,128)S(1)}, u32[]{:S(2)}, u32[]{:S(2)}) collective-permute-start(f32[512,64]{0,1:T(8,128)S(1)} %select_add_fusion.11), channel_id=1, source_target_pairs={{0,64},{16,80},{32,96},{48,112},{64,0},{80,16},{96,32},{112,48},{1... | collective-permute-start | bytes 393224 | tf_op jit(solution)/shard_map/ppermute | solution.py:52
  228.3 6.8 %collective-permute-start.25 = (f32[1024,64]{0,1:T(8,128)S(1)}, f32[1024,64]{0,1:T(8,128)S(1)}, u32[]{:S(2)}, u32[]{:S(2)}) collective-permute-start(f32[1024,64]{0,1:T(8,128)S(1)} %maximum_select_fusion.9), channel_id=1, source_target_pairs={{0,32},{16,48},{32,0},{48,16},{64,96},{80,112},{96,64},{112,80},{1... | collective-permute-start | bytes 786440 | tf_op jit(solution)/shard_map/ppermute | solution.py:52
  235.1 36.7 %collective-permute-start.26 = (f32[2048,64]{0,1:T(8,128)S(1)}, f32[2048,64]{0,1:T(8,128)S(1)}, u32[]{:S(2)}, u32[]{:S(2)}) collective-permute-start(f32[2048,64]{0,1:T(8,128)S(1)} %maximum_select_fusion.4), channel_id=1, source_target_pairs={{0,16},{16,0},{32,48},{48,32},{64,80},{80,64},{96,112},{112,96},{1... | collective-permute-start | bytes 1572872 | tf_op jit(solution)/shard_map/ppermute | solution.py:52
  236.4 10.1 %collective-permute-start.14 = (f32[64]{0:T(128)S(1)}, f32[64]{0:T(128)S(1)}, u32[]{:S(2)}, u32[]{:S(2)}) collective-permute-start(f32[64]{0:T(128)S(1)} %fusion.24), channel_id=1, source_target_pairs={{0,16},{16,0},{32,48},{48,32},{64,80},{80,64},{96,112},{112,96},{1... | collective-permute-start | bytes 776 | tf_op jit(solution)/shard_map/ppermute | solution.py:35
  254.4 8.7 %collective-permute-start.17 = (f32[64]{0:T(128)S(1)}, f32[64]{0:T(128)S(1)}, u32[]{:S(2)}, u32[]{:S(2)}) collective-permute-start(f32[64]{0:T(128)S(1)} %add.250), channel_id=1, source_target_pairs={{0,1},{1,0},{2,3},{3,2},{4,5},{5,4},{6,7},{7,6},{8,9},{9,8},{10,11... | collective-permute-start | bytes 776 | tf_op jit(solution)/shard_map/ppermute | solution.py:35
  297.6 5.0 %collective-permute-start.31 = (f32[1024,64]{0,1:T(8,128)S(1)}, f32[1024,64]{0,1:T(8,128)S(1)}, u32[]{:S(2)}, u32[]{:S(2)}) collective-permute-start(f32[1024,64]{0,1:T(8,128)S(1)} %slice_select_fusion.4), channel_id=1, source_target_pairs={{0,1},{1,0},{2,3},{3,2},{4,5},{5,4},{6,7},{7,6},{8,9},{9,8},{10,11... | collective-permute-start | bytes 786440 | tf_op jit(solution)/shard_map/ppermute | solution.py:49
  302.7 4.8 %collective-permute-start.32 = (f32[512,64]{0,1:T(8,128)S(1)}, f32[512,64]{0,1:T(8,128)S(1)}, u32[]{:S(2)}, u32[]{:S(2)}) collective-permute-start(f32[512,64]{0,1:T(8,128)S(1)} %slice_select_fusion.9), channel_id=1, source_target_pairs={{0,2},{1,3},{2,0},{3,1},{4,6},{5,7},{6,4},{7,5},{8,10},{9,11},{10,... | collective-permute-start | bytes 393224 | tf_op jit(solution)/shard_map/ppermute | solution.py:49
  325.4 8.2 %collective-permute-start.38 = (bf16[1024,64]{0,1:T(8,128)(2,1)S(1)}, bf16[1024,64]{0,1:T(8,128)(2,1)S(1)}, u32[]{:S(2)}, u32[]{:S(2)}) collective-permute-start(bf16[1024,64]{0,1:T(8,128)(2,1)S(1)} %maximum_select_fusion.10), channel_id=1, source_target_pairs={{0,1},{1,0},{2,3},{3,2},{4,5},{5,4},{6,7},{7,6},{8,9},{9,8},{10,11... | collective-permute-start | bytes 393224 | tf_op jit(solution)/shard_map/ppermute | solution.py:52
  366.2 5.0 %collective-permute-start.46 = (f32[1024,64]{0,1:T(8,128)S(1)}, f32[1024,64]{0,1:T(8,128)S(1)}, u32[]{:S(2)}, u32[]{:S(2)}) collective-permute-start(f32[1024,64]{0,1:T(8,128)S(1)} %slice_select_fusion.3), channel_id=1, source_target_pairs={{0,1},{1,0},{2,3},{3,2},{4,5},{5,4},{6,7},{7,6},{8,9},{9,8},{10,11... | collective-permute-start | bytes 786440 | tf_op jit(solution)/shard_map/ppermute | solution.py:49
  371.3 4.8 %collective-permute-start.47 = (f32[512,64]{0,1:T(8,128)S(1)}, f32[512,64]{0,1:T(8,128)S(1)}, u32[]{:S(2)}, u32[]{:S(2)}) collective-permute-start(f32[512,64]{0,1:T(8,128)S(1)} %slice_select_fusion.8), channel_id=1, source_target_pairs={{0,2},{1,3},{2,0},{3,1},{4,6},{5,7},{6,4},{7,5},{8,10},{9,11},{10,... | collective-permute-start | bytes 393224 | tf_op jit(solution)/shard_map/ppermute | solution.py:49
  395.8 7.9 %collective-permute-start.53 = (f32[1024,64]{0,1:T(8,128)S(1)}, f32[1024,64]{0,1:T(8,128)S(1)}, u32[]{:S(2)}, u32[]{:S(2)}) collective-permute-start(f32[1024,64]{0,1:T(8,128)S(1)} %maximum_select_fusion.11), channel_id=1, source_target_pairs={{0,1},{1,0},{2,3},{3,2},{4,5},{5,4},{6,7},{7,6},{8,9},{9,8},{10,11... | collective-permute-start | bytes 786440 | tf_op jit(solution)/shard_map/ppermute | solution.py:52
  (37 other events, 420.3 us)
Sparse Core Ops, SparseCore 0:
  9.0 35.7 all-gather.1

commit v2 on v1

--- a/solution.py
+++ b/solution.py
@@ -36,18 +36,31 @@
     return x
 
 
-def ring_sum(x, axis):
+def ring_sum(x, axis, halvings=1):
     n = lax.axis_size(axis)
     idx = lax.axis_index(axis)
     bits = _bits(n)
-    for k in bits:
+    split, whole = bits[:halvings], bits[halvings:]
+    for k in split:
         half = x.shape[0] // 2
         upper = (idx // k) % 2 == 1
         lo, hi = x[:half], x[half:]
         keep = jnp.where(upper, hi, lo)
         send = jnp.where(upper, lo, hi)
         x = keep + lax.ppermute(send, axis, _pairs(n, k))
-    for k in reversed(bits):
+    for k in whole:
+        x = x + lax.ppermute(x, axis, _pairs(n, k))
+    for k in reversed(split):
+        upper = (idx // k) % 2 == 1
+        other = lax.ppermute(x, axis, _pairs(n, k))
+        x = jnp.where(upper, jnp.concatenate([other, x], 0), jnp.concatenate([x, other], 0))
+    return x
+
+
+def gather_rows(x, axis):
+    n = lax.axis_size(axis)
+    idx = lax.axis_index(axis)
+    for k in _bits(n):
         upper = (idx // k) % 2 == 1
         other = lax.ppermute(x, axis, _pairs(n, k))
         x = jnp.where(upper, jnp.concatenate([other, x], 0), jnp.concatenate([x, other], 0))
@@ -55,7 +68,7 @@
 
 
 def shards(queries, landmarks, targets, ridge):
-    qhat = normalize(lax.all_gather(queries, "lm", axis=1, tiled=True))
+    qhat = normalize(gather_rows(queries.T, "lm").T)
     chat = normalize(landmarks)
     rows_dev = qhat.shape[0]
     lm_rows = chat.shape[0]

time: 418 us -> 367 us (0.88)
  waiting for transfers between devices: 204 us -> 187 us
  starting transfers between devices: 111 us -> 96.3 us
  between operations: 14.3 us -> 0.99 us
  matrix products: 65.3 us -> 59.9 us
    ppermute x0 -> x17, waiting for transfers between devices: none -> 113 us  [the longest x13 96.9 us: ring_sum(): x = x + lax.ppermute(x, axis, _pairs(n, k))]
    ppermute x18 -> x5, waiting for transfers between devices: 74.9 us -> 27.4 us  [ring_sum(): x = keep + lax.ppermute(send, axis, _pairs(n, k))]
    ppermute x18 -> x5, waiting for transfers between devices: 55.2 us -> 13.9 us  [ring_sum(): other = lax.ppermute(x, axis, _pairs(n, k))]
    all_gather x1 -> x0, waiting for transfers between devices: 33.4 us -> none  [shards(): qhat = normalize(lax.all_gather(queries, 'lm', axis=1, tiled=True))]
    ppermute x18 -> x5, starting transfers between devices: 42.8 us -> 9.4 us  [ring_sum(): other = lax.ppermute(x, axis, _pairs(n, k))]
    ppermute x0 -> x17, starting transfers between devices: none -> 33.2 us  [the longest x13 25.9 us: ring_sum(): x = x + lax.ppermute(x, axis, _pairs(n, k))]
    ppermute x18 -> x5, starting transfers between devices: 35.2 us -> 14.8 us  [ring_sum(): x = keep + lax.ppermute(send, axis, _pairs(n, k))]
    ppermute x18, waiting for transfers between devices: 40 us -> 32.9 us  [tree_sum(): x = x + lax.ppermute(x, axis, _pairs(n, k))]
  transfers between devices with their start and end apart: 55 -> 45, of which waited for: 54 -> 44; matrix products, arithmetic and copies ran while one was open for 1% -> 1% of each run, Pallas kernels for 0% -> 0%
where the time goes in v2:
time: 367 us; the launch traced here: 360 us
  waiting for transfers between devices  187 us (51%)
  starting transfers between devices  96.3 us (26%)
  matrix products  59.9 us (16%)
  other arithmetic  13.1 us (4%)
    ppermute x13, waiting for transfers between devices, ring_sum(): x = x + lax.ppermute(x, axis, _pairs(n, k))  96.9 us
    ppermute x18, starting transfers between devices, tree_sum(): x = x + lax.ppermute(x, axis, _pairs(n, k))  38.8 us
    ppermute x18, waiting for transfers between devices, tree_sum(): x = x + lax.ppermute(x, axis, _pairs(n, k))  32.9 us
    ppermute x5, waiting for transfers between devices, ring_sum(): x = keep + lax.ppermute(send, axis, _pairs(n, k))  27.4 us
    ppermute x13, starting transfers between devices, ring_sum(): x = x + lax.ppermute(x, axis, _pairs(n, k))  25.9 us
    dot_general x2, matrix products, shards(): image_part = jnp.dot(kernel, rounded, preferred_element_type=jnp.float32)  22.3 us
    dot_general x4, matrix products, tile_rows(): scores = jnp.dot(block, chat.T, preferred_element_type=jnp.float32)  17.1 us
    ppermute x4, waiting for transfers between devices, gather_rows(): other = lax.ppermute(x, axis, _pairs(n, k))  15.7 us
  transfers between devices with their start and end apart: 45, of which 44 were waited for; matrix products, arithmetic and copies ran while one was open for 1% of the time, Pallas kernels for 0%

profile of v2, /device:TPU:1, one launch (start us, length us, event | category | flops | bytes accessed | tf_op | source)
XLA Modules:
  0.0 359.5 jit_solution(14618085207103077565)
XLA Ops:
  19.9 8.3 %collective-permute-done.3 = bf16[128,2048]{1,0:T(8,128)(2,1)S(1)} collective-permute-done((bf16[128,2048]{1,0:T(8,128)(2,1)S(1)}, bf16[128,2048]{1,0:T(8,128)(2,1)S(1)}, u32[]{:S(2)}, u32[]{:S(2)}) %collective-permute-start.3) | collective-permute-done | bytes 524320 | tf_op jit(solution)/shard_map/ppermute | solution.py:65
  30.3 21.7 %while.13 = (s32[]{:T(128)}, bf16[4,512,4096]{2,1,0:T(8,128)(2,1)}, f32[4,4096]{1,0:T(4,128)S(1)}, bf16[4,512,256]{2,1,0:T(8,128)(2,1)}, bf16[4096,256]{1,0:T(8,128)(2,1)S(1)}, /*index=5*/s32[]{:T(128)}, s32[]{:T(128)}) while((s32[]{:T(128)}, bf16[4,512,4096]{2,1,0:T(8,128)(2,1)}, f32[4,4096]{1,0:T(4,128)S(1)}, ...), condition=%wide.region_4.5_spmd, body=%wide.region_2.4_spmd.sunk | while | flops 1084223488 | bytes 14992465 | solution.py:87
  52.0 8.8 %fusion.30 = f32[4096,64]{0,1:T(8,128)S(1)} fusion(bf16[2048,64]{0,1:T(8,128)(2,1)S(1)} %copy-done, bf16[2048,4096]{1,0:T(8,128)(2,1)} %bitcast.38), kind=kOutput, calls=%fused_computation.79 | convolution fusion | flops 1073741824 | bytes 18087936 | tf_op jit(solution)/shard_map/dot_general | solution.py:89
  62.6 10.7 %collective-permute-done.4 = f32[2048,65]{0,1:T(8,128)S(1)} collective-permute-done((f32[2048,65]{0,1:T(8,128)S(1)}, f32[2048,65]{0,1:T(8,128)S(1)}, u32[]{:S(2)}, u32[]{:S(2)}) %collective-permute-start.4) | collective-permute-done | bytes 532512 | tf_op jit(solution)/shard_map/ppermute | solution.py:50
  76.7 12.6 %collective-permute-done.5 = f32[2048,65]{0,1:T(8,128)S(1)} collective-permute-done((f32[2048,65]{0,1:T(8,128)S(1)}, f32[2048,65]{0,1:T(8,128)S(1)}, u32[]{:S(2)}, u32[]{:S(2)}) %collective-permute-start.5) | collective-permute-done | bytes 532512 | tf_op jit(solution)/shard_map/ppermute | solution.py:52
  92.2 10.2 %collective-permute-done.6 = f32[2048,65]{0,1:T(8,128)S(1)} collective-permute-done((f32[2048,65]{0,1:T(8,128)S(1)}, f32[2048,65]{0,1:T(8,128)S(1)}, u32[]{:S(2)}, u32[]{:S(2)}) %collective-permute-start.6) | collective-permute-done | bytes 532512 | tf_op jit(solution)/shard_map/ppermute | solution.py:52
  102.7 10.5 %collective-permute-done.7 = f32[2048,65]{0,1:T(8,128)S(1)} collective-permute-done((f32[2048,65]{0,1:T(8,128)S(1)}, f32[2048,65]{0,1:T(8,128)S(1)}, u32[]{:S(2)}, u32[]{:S(2)}) %collective-permute-start.7) | collective-permute-done | bytes 532512 | tf_op jit(solution)/shard_map/ppermute | solution.py:55
  113.5 11.1 %fusion.20 = f32[2048,64]{0,1:T(8,128)S(1)} fusion(bf16[2048,4096]{1,0:T(8,128)(2,1)} %bitcast.39, f32[4096,65]{0,1:T(8,128)S(1)} %maximum_select_fusion, f32[64]{0:T(128)S(1)} %copy-done.3, f32[4096]{0:T(1024)S(1)} %bitcast.50), kind=kOutput, calls=%fused_computation.53 | convolution fusion | flops 1074790400 | bytes 18366976 | tf_op jit(solution)/shard_map/dot_general | solution.py:102
  125.1 5.3 %collective-permute-start.8 = (f32[1024,65]{0,1:T(8,128)S(1)}, f32[1024,65]{0,1:T(8,128)S(1)}, u32[]{:S(2)}, u32[]{:S(2)}) collective-permute-start(f32[1024,65]{0,1:T(8,128)S(1)} %slice_select_fusion.1), channel_id=1, source_target_pairs={{0,1},{1,0},{2,3},{3,2},{4,5},{5,4},{6,7},{7,6},{8,9},{9,8},{10,11... | collective-permute-start | bytes 798728 | tf_op jit(solution)/shard_map/ppermute | solution.py:50
  133.0 7.0 %collective-permute-done.9 = f32[1024,65]{0,1:T(8,128)S(1)} collective-permute-done((f32[1024,65]{0,1:T(8,128)S(1)}, f32[1024,65]{0,1:T(8,128)S(1)}, u32[]{:S(2)}, u32[]{:S(2)}) %collective-permute-start.9) | collective-permute-done | bytes 266272 | tf_op jit(solution)/shard_map/ppermute | solution.py:52
  141.4 6.0 %collective-permute-done.10 = f32[1024,65]{0,1:T(8,128)S(1)} collective-permute-done((f32[1024,65]{0,1:T(8,128)S(1)}, f32[1024,65]{0,1:T(8,128)S(1)}, u32[]{:S(2)}, u32[]{:S(2)}) %collective-permute-start.10) | collective-permute-done | bytes 266272 | tf_op jit(solution)/shard_map/ppermute | solution.py:52
  150.4 5.1 %collective-permute-done.11 = f32[1024,65]{0,1:T(8,128)S(1)} collective-permute-done((f32[1024,65]{0,1:T(8,128)S(1)}, f32[1024,65]{0,1:T(8,128)S(1)}, u32[]{:S(2)}, u32[]{:S(2)}) %collective-permute-start.11) | collective-permute-done | bytes 266272 | tf_op jit(solution)/shard_map/ppermute | solution.py:52
  163.4 13.1 %collective-permute-done.20 = f32[2048,64]{0,1:T(8,128)S(1)} collective-permute-done((f32[2048,64]{0,1:T(8,128)S(1)}, f32[2048,64]{0,1:T(8,128)S(1)}, u32[]{:S(2)}, u32[]{:S(2)}) %collective-permute-start.20) | collective-permute-done | bytes 524320 | tf_op jit(solution)/shard_map/ppermute | solution.py:50
  176.7 13.7 %collective-permute-done.21 = f32[2048,64]{0,1:T(8,128)S(1)} collective-permute-done((f32[2048,64]{0,1:T(8,128)S(1)}, f32[2048,64]{0,1:T(8,128)S(1)}, u32[]{:S(2)}, u32[]{:S(2)}) %collective-permute-start.21) | collective-permute-done | bytes 524320 | tf_op jit(solution)/shard_map/ppermute | solution.py:52
  193.3 10.2 %collective-permute-done.22 = f32[2048,64]{0,1:T(8,128)S(1)} collective-permute-done((f32[2048,64]{0,1:T(8,128)S(1)}, f32[2048,64]{0,1:T(8,128)S(1)}, u32[]{:S(2)}, u32[]{:S(2)}) %collective-permute-start.22) | collective-permute-done | bytes 524320 | tf_op jit(solution)/shard_map/ppermute | solution.py:52
  205.1 9.1 %collective-permute-done.13 = f32[64]{0:T(128)S(1)} collective-permute-done((f32[64]{0:T(128)S(1)}, f32[64]{0:T(128)S(1)}, u32[]{:S(2)}, u32[]{:S(2)}) %collective-permute-start.13) | collective-permute-done | bytes 288 | tf_op jit(solution)/shard_map/ppermute | solution.py:35
  222.0 6.2 %collective-permute-start.16 = (f32[64]{0:T(128)S(1)}, f32[64]{0:T(128)S(1)}, u32[]{:S(2)}, u32[]{:S(2)}) collective-permute-start(f32[64]{0:T(128)S(1)} %add.220), channel_id=1, source_target_pairs={{0,1},{1,0},{2,3},{3,2},{4,5},{5,4},{6,7},{7,6},{8,9},{9,8},{10,11... | collective-permute-start | bytes 776 | tf_op jit(solution)/shard_map/ppermute | solution.py:35
  252.7 11.1 %fusion.17 = f32[2048,64]{0,1:T(8,128)S(1)} fusion(bf16[2048,4096]{1,0:T(8,128)(2,1)} %bitcast.40, f32[4096,64]{0,1:T(8,128)S(1)} %get-tuple-element.60), kind=kOutput, calls=%fused_computation.49 | convolution fusion | flops 1074003968 | bytes 18350080 | tf_op jit(solution)/shard_map/dot_general | solution.py:102
  270.2 6.3 %collective-permute-done.29 = f32[1024,64]{0,1:T(8,128)S(1)} collective-permute-done((f32[1024,64]{0,1:T(8,128)S(1)}, f32[1024,64]{0,1:T(8,128)S(1)}, u32[]{:S(2)}, u32[]{:S(2)}) %collective-permute-start.29) | collective-permute-done | bytes 262176 | tf_op jit(solution)/shard_map/ppermute | solution.py:52
  277.9 5.3 %collective-permute-done.30 = f32[1024,64]{0,1:T(8,128)S(1)} collective-permute-done((f32[1024,64]{0,1:T(8,128)S(1)}, f32[1024,64]{0,1:T(8,128)S(1)}, u32[]{:S(2)}, u32[]{:S(2)}) %collective-permute-start.30) | collective-permute-done | bytes 262176 | tf_op jit(solution)/shard_map/ppermute | solution.py:52
  286.2 4.4 %collective-permute-done.31 = f32[1024,64]{0,1:T(8,128)S(1)} collective-permute-done((f32[1024,64]{0,1:T(8,128)S(1)}, f32[1024,64]{0,1:T(8,128)S(1)}, u32[]{:S(2)}, u32[]{:S(2)}) %collective-permute-start.31) | collective-permute-done | bytes 262176 | tf_op jit(solution)/shard_map/ppermute | solution.py:52
  321.9 5.3 %fusion.14 = f32[2048,64]{0,1:T(8,128)S(1)} fusion(bf16[2048,4096]{1,0:T(8,128)(2,1)S(1)} %bitcast.47, f32[4096,64]{0,1:T(8,128)S(1)} %get-tuple-element.60, f32[64]{0:T(128)S(1)} %add_divide_fusion.2, f32[64]{0:T(128)S(1)} %add_divide_fusion.3, f32[4096,65]{0,1:T(8,128)S(1)} %maximum_select_fusion, f32[64]{0:T(128)S(1)} %copy-done.3, f32[4096]{0:T(1024)S(1)} %bitcast.55), kind=kOutput, calls=%fused_computation.42 | convolution fusion | flops 1075576832 | bytes 19416576 | tf_op jit(solution)/shard_map/dot_general | solution.py:131
  333.6 6.3 %collective-permute-done.41 = f32[1024,64]{0,1:T(8,128)S(1)} collective-permute-done((f32[1024,64]{0,1:T(8,128)S(1)}, f32[1024,64]{0,1:T(8,128)S(1)}, u32[]{:S(2)}, u32[]{:S(2)}) %collective-permute-start.41) | collective-permute-done | bytes 262176 | tf_op jit(solution)/shard_map/ppermute | solution.py:52
  341.3 5.3 %collective-permute-done.42 = f32[1024,64]{0,1:T(8,128)S(1)} collective-permute-done((f32[1024,64]{0,1:T(8,128)S(1)}, f32[1024,64]{0,1:T(8,128)S(1)}, u32[]{:S(2)}, u32[]{:S(2)}) %collective-permute-start.42) | collective-permute-done | bytes 262176 | tf_op jit(solution)/shard_map/ppermute | solution.py:52
  (175 shorter events, 166.4 us)
Async XLA Ops:
  8.3 6.7 %collective-permute-start.2 = (bf16[64,2048]{1,0:T(8,128)(2,1)S(1)}, bf16[64,2048]{1,0:T(8,128)(2,1)S(1)}, u32[]{:S(2)}, u32[]{:S(2)}) collective-permute-start(bf16[64,2048]{1,0:T(8,128)(2,1)S(1)} %maximum_select_fusion.7), channel_id=1, source_target_pairs={{0,4},{1,5},{2,6},{3,7},{4,0},{5,1},{6,2},{7,3},{8,12},{9,13},{10,... | collective-permute-start | bytes 786440 | tf_op jit(solution)/shard_map/ppermute | solution.py:65
  15.1 13.1 %collective-permute-start.3 = (bf16[128,2048]{1,0:T(8,128)(2,1)S(1)}, bf16[128,2048]{1,0:T(8,128)(2,1)S(1)}, u32[]{:S(2)}, u32[]{:S(2)}) collective-permute-start(bf16[128,2048]{1,0:T(8,128)(2,1)S(1)} %maximum_select_fusion.4), channel_id=1, source_target_pairs={{0,8},{1,9},{2,10},{3,11},{4,12},{5,13},{6,14},{7,15},{8,0},{9,1},... | collective-permute-start | bytes 1572872 | tf_op jit(solution)/shard_map/ppermute | solution.py:65
  60.9 12.4 %collective-permute-start.4 = (f32[2048,65]{0,1:T(8,128)S(1)}, f32[2048,65]{0,1:T(8,128)S(1)}, u32[]{:S(2)}, u32[]{:S(2)}) collective-permute-start(f32[2048,65]{0,1:T(8,128)S(1)} %broadcast_select_fusion), channel_id=1, source_target_pairs={{0,16},{16,0},{32,48},{48,32},{64,80},{80,64},{96,112},{112,96},{1... | collective-permute-start | bytes 1597448 | tf_op jit(solution)/shard_map/ppermute | solution.py:50
  73.4 15.9 %collective-permute-start.5 = (f32[2048,65]{0,1:T(8,128)S(1)}, f32[2048,65]{0,1:T(8,128)S(1)}, u32[]{:S(2)}, u32[]{:S(2)}) collective-permute-start(f32[2048,65]{0,1:T(8,128)S(1)} %select_add_fusion), channel_id=1, source_target_pairs={{0,32},{16,48},{32,0},{48,16},{64,96},{80,112},{96,64},{112,80},{1... | collective-permute-start | bytes 1597448 | tf_op jit(solution)/shard_map/ppermute | solution.py:52
  89.4 13.0 %collective-permute-start.6 = (f32[2048,65]{0,1:T(8,128)S(1)}, f32[2048,65]{0,1:T(8,128)S(1)}, u32[]{:S(2)}, u32[]{:S(2)}) collective-permute-start(f32[2048,65]{0,1:T(8,128)S(1)} %add.207), channel_id=1, source_target_pairs={{0,64},{16,80},{32,96},{48,112},{64,0},{80,16},{96,32},{112,48},{1... | collective-permute-start | bytes 1597448 | tf_op jit(solution)/shard_map/ppermute | solution.py:52
  102.5 10.8 %collective-permute-start.7 = (f32[2048,65]{0,1:T(8,128)S(1)}, f32[2048,65]{0,1:T(8,128)S(1)}, u32[]{:S(2)}, u32[]{:S(2)}) collective-permute-start(f32[2048,65]{0,1:T(8,128)S(1)} %add.208), channel_id=1, source_target_pairs={{0,16},{16,0},{32,48},{48,32},{64,80},{80,64},{96,112},{112,96},{1... | collective-permute-start | bytes 1597448 | tf_op jit(solution)/shard_map/ppermute | solution.py:55
  125.1 6.5 %collective-permute-start.8 = (f32[1024,65]{0,1:T(8,128)S(1)}, f32[1024,65]{0,1:T(8,128)S(1)}, u32[]{:S(2)}, u32[]{:S(2)}) collective-permute-start(f32[1024,65]{0,1:T(8,128)S(1)} %slice_select_fusion.1), channel_id=1, source_target_pairs={{0,1},{1,0},{2,3},{3,2},{4,5},{5,4},{6,7},{7,6},{8,9},{9,8},{10,11... | collective-permute-start | bytes 798728 | tf_op jit(solution)/shard_map/ppermute | solution.py:50
  131.7 8.3 %collective-permute-start.9 = (f32[1024,65]{0,1:T(8,128)S(1)}, f32[1024,65]{0,1:T(8,128)S(1)}, u32[]{:S(2)}, u32[]{:S(2)}) collective-permute-start(f32[1024,65]{0,1:T(8,128)S(1)} %select_add_fusion.2), channel_id=1, source_target_pairs={{0,2},{1,3},{2,0},{3,1},{4,6},{5,7},{6,4},{7,5},{8,10},{9,11},{10,... | collective-permute-start | bytes 798728 | tf_op jit(solution)/shard_map/ppermute | solution.py:52
  140.0 7.4 %collective-permute-start.10 = (f32[1024,65]{0,1:T(8,128)S(1)}, f32[1024,65]{0,1:T(8,128)S(1)}, u32[]{:S(2)}, u32[]{:S(2)}) collective-permute-start(f32[1024,65]{0,1:T(8,128)S(1)} %add.214), channel_id=1, source_target_pairs={{0,4},{1,5},{2,6},{3,7},{4,0},{5,1},{6,2},{7,3},{8,12},{9,13},{10,... | collective-permute-start | bytes 798728 | tf_op jit(solution)/shard_map/ppermute | solution.py:52
  147.4 8.1 %collective-permute-start.11 = (f32[1024,65]{0,1:T(8,128)S(1)}, f32[1024,65]{0,1:T(8,128)S(1)}, u32[]{:S(2)}, u32[]{:S(2)}) collective-permute-start(f32[1024,65]{0,1:T(8,128)S(1)} %add.215), channel_id=1, source_target_pairs={{0,8},{1,9},{2,10},{3,11},{4,12},{5,13},{6,14},{7,15},{8,0},{9,1},... | collective-permute-start | bytes 798728 | tf_op jit(solution)/shard_map/ppermute | solution.py:52
  163.3 13.2 %collective-permute-start.20 = (f32[2048,64]{0,1:T(8,128)S(1)}, f32[2048,64]{0,1:T(8,128)S(1)}, u32[]{:S(2)}, u32[]{:S(2)}) collective-permute-start(f32[2048,64]{0,1:T(8,128)S(1)} %slice_select_fusion), channel_id=1, source_target_pairs={{0,16},{16,0},{32,48},{48,32},{64,80},{80,64},{96,112},{112,96},{1... | collective-permute-start | bytes 1572872 | tf_op jit(solution)/shard_map/ppermute | solution.py:50
  176.6 13.8 %collective-permute-start.21 = (f32[2048,64]{0,1:T(8,128)S(1)}, f32[2048,64]{0,1:T(8,128)S(1)}, u32[]{:S(2)}, u32[]{:S(2)}) collective-permute-start(f32[2048,64]{0,1:T(8,128)S(1)} %select_add_fusion.1), channel_id=1, source_target_pairs={{0,32},{16,48},{32,0},{48,16},{64,96},{80,112},{96,64},{112,80},{1... | collective-permute-start | bytes 1572872 | tf_op jit(solution)/shard_map/ppermute | solution.py:52
  190.5 13.0 %collective-permute-start.22 = (f32[2048,64]{0,1:T(8,128)S(1)}, f32[2048,64]{0,1:T(8,128)S(1)}, u32[]{:S(2)}, u32[]{:S(2)}) collective-permute-start(f32[2048,64]{0,1:T(8,128)S(1)} %add.226), channel_id=1, source_target_pairs={{0,64},{16,80},{32,96},{48,112},{64,0},{80,16},{96,32},{112,48},{1... | collective-permute-start | bytes 1572872 | tf_op jit(solution)/shard_map/ppermute | solution.py:52
  203.5 34.5 %collective-permute-start.23 = (f32[2048,64]{0,1:T(8,128)S(1)}, f32[2048,64]{0,1:T(8,128)S(1)}, u32[]{:S(2)}, u32[]{:S(2)}) collective-permute-start(f32[2048,64]{0,1:T(8,128)S(1)} %add.227), channel_id=1, source_target_pairs={{0,16},{16,0},{32,48},{48,32},{64,80},{80,64},{96,112},{112,96},{1... | collective-permute-start | bytes 1572872 | tf_op jit(solution)/shard_map/ppermute | solution.py:55
  203.7 10.5 %collective-permute-start.13 = (f32[64]{0:T(128)S(1)}, f32[64]{0:T(128)S(1)}, u32[]{:S(2)}, u32[]{:S(2)}) collective-permute-start(f32[64]{0:T(128)S(1)} %fusion.25), channel_id=1, source_target_pairs={{0,16},{16,0},{32,48},{48,32},{64,80},{80,64},{96,112},{112,96},{1... | collective-permute-start | bytes 776 | tf_op jit(solution)/shard_map/ppermute | solution.py:35
  222.0 7.0 %collective-permute-start.16 = (f32[64]{0:T(128)S(1)}, f32[64]{0:T(128)S(1)}, u32[]{:S(2)}, u32[]{:S(2)}) collective-permute-start(f32[64]{0:T(128)S(1)} %add.220), channel_id=1, source_target_pairs={{0,1},{1,0},{2,3},{3,2},{4,5},{5,4},{6,7},{7,6},{8,9},{9,8},{10,11... | collective-permute-start | bytes 776 | tf_op jit(solution)/shard_map/ppermute | solution.py:35
  263.9 5.0 %collective-permute-start.28 = (f32[1024,64]{0,1:T(8,128)S(1)}, f32[1024,64]{0,1:T(8,128)S(1)}, u32[]{:S(2)}, u32[]{:S(2)}) collective-permute-start(f32[1024,64]{0,1:T(8,128)S(1)} %slice_select_fusion.3), channel_id=1, source_target_pairs={{0,1},{1,0},{2,3},{3,2},{4,5},{5,4},{6,7},{7,6},{8,9},{9,8},{10,11... | collective-permute-start | bytes 786440 | tf_op jit(solution)/shard_map/ppermute | solution.py:50
  268.9 7.6 %collective-permute-start.29 = (f32[1024,64]{0,1:T(8,128)S(1)}, f32[1024,64]{0,1:T(8,128)S(1)}, u32[]{:S(2)}, u32[]{:S(2)}) collective-permute-start(f32[1024,64]{0,1:T(8,128)S(1)} %select_add_fusion.4), channel_id=1, source_target_pairs={{0,2},{1,3},{2,0},{3,1},{4,6},{5,7},{6,4},{7,5},{8,10},{9,11},{10,... | collective-permute-start | bytes 786440 | tf_op jit(solution)/shard_map/ppermute | solution.py:52
  276.5 6.7 %collective-permute-start.30 = (f32[1024,64]{0,1:T(8,128)S(1)}, f32[1024,64]{0,1:T(8,128)S(1)}, u32[]{:S(2)}, u32[]{:S(2)}) collective-permute-start(f32[1024,64]{0,1:T(8,128)S(1)} %add.235), channel_id=1, source_target_pairs={{0,4},{1,5},{2,6},{3,7},{4,0},{5,1},{6,2},{7,3},{8,12},{9,13},{10,... | collective-permute-start | bytes 786440 | tf_op jit(solution)/shard_map/ppermute | solution.py:52
  283.3 7.4 %collective-permute-start.31 = (f32[1024,64]{0,1:T(8,128)S(1)}, f32[1024,64]{0,1:T(8,128)S(1)}, u32[]{:S(2)}, u32[]{:S(2)}) collective-permute-start(f32[1024,64]{0,1:T(8,128)S(1)} %add.236), channel_id=1, source_target_pairs={{0,8},{1,9},{2,10},{3,11},{4,12},{5,13},{6,14},{7,15},{8,0},{9,1},... | collective-permute-start | bytes 786440 | tf_op jit(solution)/shard_map/ppermute | solution.py:52
  327.2 5.0 %collective-permute-start.40 = (f32[1024,64]{0,1:T(8,128)S(1)}, f32[1024,64]{0,1:T(8,128)S(1)}, u32[]{:S(2)}, u32[]{:S(2)}) collective-permute-start(f32[1024,64]{0,1:T(8,128)S(1)} %slice_select_fusion.2), channel_id=1, source_target_pairs={{0,1},{1,0},{2,3},{3,2},{4,5},{5,4},{6,7},{7,6},{8,9},{9,8},{10,11... | collective-permute-start | bytes 786440 | tf_op jit(solution)/shard_map/ppermute | solution.py:50
  332.3 7.6 %collective-permute-start.41 = (f32[1024,64]{0,1:T(8,128)S(1)}, f32[1024,64]{0,1:T(8,128)S(1)}, u32[]{:S(2)}, u32[]{:S(2)}) collective-permute-start(f32[1024,64]{0,1:T(8,128)S(1)} %select_add_fusion.3), channel_id=1, source_target_pairs={{0,2},{1,3},{2,0},{3,1},{4,6},{5,7},{6,4},{7,5},{8,10},{9,11},{10,... | collective-permute-start | bytes 786440 | tf_op jit(solution)/shard_map/ppermute | solution.py:52
  339.9 6.7 %collective-permute-start.42 = (f32[1024,64]{0,1:T(8,128)S(1)}, f32[1024,64]{0,1:T(8,128)S(1)}, u32[]{:S(2)}, u32[]{:S(2)}) collective-permute-start(f32[1024,64]{0,1:T(8,128)S(1)} %add.248), channel_id=1, source_target_pairs={{0,4},{1,5},{2,6},{3,7},{4,0},{5,1},{6,2},{7,3},{8,12},{9,13},{10,... | collective-permute-start | bytes 786440 | tf_op jit(solution)/shard_map/ppermute | solution.py:52
  346.7 7.4 %collective-permute-start.43 = (f32[1024,64]{0,1:T(8,128)S(1)}, f32[1024,64]{0,1:T(8,128)S(1)}, u32[]{:S(2)}, u32[]{:S(2)}) collective-permute-start(f32[1024,64]{0,1:T(8,128)S(1)} %add.249), channel_id=1, source_target_pairs={{0,8},{1,9},{2,10},{3,11},{4,12},{5,13},{6,14},{7,15},{8,0},{9,1},... | collective-permute-start | bytes 786440 | tf_op jit(solution)/shard_map/ppermute | solution.py:52
  (33 other events, 527.1 us)

commit v3 on v2

--- a/solution.py
+++ b/solution.py
@@ -16,8 +16,23 @@
     return (values * scale).astype(jnp.bfloat16)
 
 
-def _pairs(n, k):
+RING_HIGH = {"dp": (8, 2), "lm": (16, 8)}
+
+
+def _pairs(n, k, axis=None):
+    size, high = RING_HIGH.get(axis, (0, 0))
+    if n == size and k == high:
+        lo = k // 2
+        return [(i, i + (3 - 2 * ((i // lo) % 4)) * lo) for i in range(n)]
     return [(i, i ^ k) for i in range(n)]
+
+
+def _order(n, axis):
+    bits = _bits(n)
+    size, high = RING_HIGH.get(axis, (0, 0))
+    if n == size and axis == "dp":
+        bits = [high] + [k for k in bits if k != high]
+    return bits
 
 
 def _bits(n):
@@ -32,14 +47,14 @@
 def tree_sum(x, axis):
     n = lax.axis_size(axis)
     for k in _bits(n):
-        x = x + lax.ppermute(x, axis, _pairs(n, k))
+        x = x + lax.ppermute(x, axis, _pairs(n, k, axis))
     return x
 
 
 def ring_sum(x, axis, halvings=1):
     n = lax.axis_size(axis)
     idx = lax.axis_index(axis)
-    bits = _bits(n)
+    bits = _order(n, axis)
     split, whole = bits[:halvings], bits[halvings:]
     for k in split:
         half = x.shape[0] // 2
@@ -47,12 +62,12 @@
         lo, hi = x[:half], x[half:]
         keep = jnp.where(upper, hi, lo)
         send = jnp.where(upper, lo, hi)
-        x = keep + lax.ppermute(send, axis, _pairs(n, k))
+        x = keep + lax.ppermute(send, axis, _pairs(n, k, axis))
     for k in whole:
-        x = x + lax.ppermute(x, axis, _pairs(n, k))
+        x = x + lax.ppermute(x, axis, _pairs(n, k, axis))
     for k in reversed(split):
         upper = (idx // k) % 2 == 1
-        other = lax.ppermute(x, axis, _pairs(n, k))
+        other = lax.ppermute(x, axis, _pairs(n, k, axis))
         x = jnp.where(upper, jnp.concatenate([other, x], 0), jnp.concatenate([x, other], 0))
     return x
 
@@ -62,7 +77,7 @@
     idx = lax.axis_index(axis)
     for k in _bits(n):
         upper = (idx // k) % 2 == 1
-        other = lax.ppermute(x, axis, _pairs(n, k))
+        other = lax.ppermute(x, axis, _pairs(n, k, axis))
         x = jnp.where(upper, jnp.concatenate([other, x], 0), jnp.concatenate([x, other], 0))
     return x
 
@@ -89,7 +104,8 @@
     rhs_part = lax.dot_general(
         kernel, targets, (((0,), (0,)), ((), ())), preferred_element_type=jnp.float32
     )
-    stacked = ring_sum(jnp.concatenate([rhs_part, jnp.sum(column_sq, axis=0)[:, None]], 1), "dp")
+    sq_part = jnp.sum(column_sq, axis=0)
+    stacked = ring_sum(jnp.concatenate([rhs_part, sq_part[:, None]], 1), "dp")
     rhs = stacked[:, :n_tg] / total_rows
     precond = stacked[:, n_tg:] / total_rows + ridge[None, :]
     coefficients = jnp.zeros_like(rhs)
@@ -98,7 +114,7 @@
     norm_part = jnp.sum(residual * direction, axis=0)
     norm_now = None
     for step in range(ITERS):
-        rounded = direction.astype(jnp.bfloat16)
+        rounded = lax.optimization_barrier(direction.astype(jnp.bfloat16))
         image_part = jnp.dot(kernel, rounded, preferred_element_type=jnp.float32)
         if norm_now is None:
             extra = jnp.zeros((rows_dev, 1), jnp.float32).at[:n_tg, 0].set(norm_part)
@@ -109,15 +125,21 @@
             query_image = ring_sum(image_part, "lm")
         back_part = lax.dot_general(
             kernel,
-            query_image.astype(jnp.bfloat16),
+            lax.optimization_barrier(query_image.astype(jnp.bfloat16)),
             (((0,), (0,)), ((), ())),
             preferred_element_type=jnp.float32,
         )
         dot_part = jnp.sum(direction * back_part, axis=0) / total_rows + jnp.where(
             first_dp, ridge * jnp.sum(direction * direction, axis=0), 0.0
         )
-        dot_all = tree_sum(tree_sum(dot_part, "dp"), "lm")
-        back = ring_sum(back_part, "dp")
+        if step + 1 < ITERS:
+            extra = jnp.zeros((lm_rows, 1), jnp.float32).at[:n_tg, 0].set(dot_part)
+            summed = ring_sum(jnp.concatenate([back_part, extra], 1), "dp")
+            back = summed[:, :n_tg]
+            dot_all = tree_sum(summed[:n_tg, n_tg], "lm")
+        else:
+            back = ring_sum(back_part, "dp")
+            dot_all = tree_sum(tree_sum(dot_part, "dp"), "lm")
         image = back / total_rows + ridge[None, :] * direction
         alpha = norm_now / dot_all
         coefficients = coefficients + alpha[None, :] * direction
@@ -127,7 +149,7 @@
             norm_next = tree_sum(jnp.sum(residual * scaled, axis=0), "lm")
             direction = scaled + (norm_next / norm_now)[None, :] * direction
             norm_now = norm_next
-    rounded_coef = coefficients.astype(jnp.bfloat16)
+    rounded_coef = lax.optimization_barrier(coefficients.astype(jnp.bfloat16))
     return ring_sum(jnp.dot(kernel, rounded_coef, preferred_element_type=jnp.float32), "lm")
 
 

time: 367 us -> 359 us (0.978)
  starting transfers between devices: 96.3 us -> 84.8 us
    ppermute x45 -> x42, starting transfers between devices: 96.3 us -> 84.8 us  [the longest x15 27.6 us: tree_sum(): x = x + lax.ppermute(x, axis, _pairs(n, k, axis))]
    dot_general x2, matrix products: 22.3 us -> 16.1 us  [shards(): image_part = jnp.dot(kernel, rounded, preferred_element_type=jnp.float32)]
    dot_general x2, matrix products: 6.55 us -> 12.3 us  [shards(): lax.dot_general(kernel, lax.optimization_barrier(query_image.astype(jnp.b...]
    ppermute x45 -> x42, waiting for transfers between devices: 187 us -> 190 us  [the longest x13 101 us: ring_sum(): x = x + lax.ppermute(x, axis, _pairs(n, k, axis))]
  transfers between devices with their start and end apart: 45 -> 42, of which waited for: 44 -> 42; matrix products, arithmetic and copies ran while one was open for 1% -> 1% of each run, Pallas kernels for 0% -> 0%
where the time goes in v3:
time: 359 us; the launch traced here: 352 us
  waiting for transfers between devices  190 us (53%)
  starting transfers between devices  84.8 us (24%)
  matrix products  59.4 us (17%)
  other arithmetic  14 us (4%)
    ppermute x13, waiting for transfers between devices, ring_sum(): x = x + lax.ppermute(x, axis, _pairs(n, k, axis))  101 us
    ppermute x5, waiting for transfers between devices, ring_sum(): x = keep + lax.ppermute(send, axis, _pairs(n, k, axis))  28.3 us
    ppermute x15, starting transfers between devices, tree_sum(): x = x + lax.ppermute(x, axis, _pairs(n, k, axis))  27.6 us
    ppermute x5, waiting for transfers between devices, ring_sum(): other = lax.ppermute(x, axis, _pairs(n, k, axis))  23.6 us
    ppermute x15, waiting for transfers between devices, tree_sum(): x = x + lax.ppermute(x, axis, _pairs(n, k, axis))  22.3 us
    ppermute x5, starting transfers between devices, ring_sum(): x = keep + lax.ppermute(send, axis, _pairs(n, k, axis))  19.5 us
    ppermute x13, starting transfers between devices, ring_sum(): x = x + lax.ppermute(x, axis, _pairs(n, k, axis))  17.4 us
    dot_general x4, matrix products, tile_rows(): scores = jnp.dot(block, chat.T, preferred_element_type=jnp.float32)  17 us
  transfers between devices with their start and end apart: 42, of which 42 were waited for; matrix products, arithmetic and copies ran while one was open for 1% of the time, Pallas kernels for 0%

profile of v3, /device:TPU:1, one launch (start us, length us, event | category | flops | bytes accessed | tf_op | source)
XLA Modules:
  0.0 352.2 jit_solution(6161821976095715416)
XLA Ops:
  19.7 8.4 %collective-permute-done.3 = bf16[128,2048]{1,0:T(8,128)(2,1)S(1)} collective-permute-done((bf16[128,2048]{1,0:T(8,128)(2,1)S(1)}, bf16[128,2048]{1,0:T(8,128)(2,1)S(1)}, u32[]{:S(2)}, u32[]{:S(2)}) %collective-permute-start.3) | collective-permute-done | bytes 524320 | tf_op jit(solution)/shard_map/ppermute | solution.py:80
  30.2 21.6 %while.14 = (s32[]{:T(128)}, bf16[4,512,4096]{2,1,0:T(8,128)(2,1)}, f32[4,4096]{1,0:T(4,128)S(1)}, bf16[4,512,256]{2,1,0:T(8,128)(2,1)}, bf16[4096,256]{1,0:T(8,128)(2,1)S(1)}, /*index=5*/s32[]{:T(128)}, s32[]{:T(128)}) while((s32[]{:T(128)}, bf16[4,512,4096]{2,1,0:T(8,128)(2,1)}, f32[4,4096]{1,0:T(4,128)S(1)}, ...), condition=%wide.region_4.5_spmd, body=%wide.region_2.4_spmd.sunk | while | flops 1084223488 | bytes 14992465 | solution.py:102
  51.9 8.8 %fusion.24 = f32[4096,64]{0,1:T(8,128)S(1)} fusion(bf16[2048,64]{0,1:T(8,128)(2,1)S(1)} %copy-done, bf16[2048,4096]{1,0:T(8,128)(2,1)} %bitcast.49), kind=kOutput, calls=%fused_computation.79 | convolution fusion | flops 1073741824 | bytes 18087936 | tf_op jit(solution)/shard_map/dot_general | solution.py:104
  64.5 10.8 %collective-permute-done.4 = f32[2048,65]{0,1:T(8,128)S(1)} collective-permute-done((f32[2048,65]{0,1:T(8,128)S(1)}, f32[2048,65]{0,1:T(8,128)S(1)}, u32[]{:S(2)}, u32[]{:S(2)}) %collective-permute-start.4) | collective-permute-done | bytes 532512 | tf_op jit(solution)/shard_map/ppermute | solution.py:65
  75.6 11.4 %collective-permute-done.5 = f32[2048,65]{0,1:T(8,128)S(1)} collective-permute-done((f32[2048,65]{0,1:T(8,128)S(1)}, f32[2048,65]{0,1:T(8,128)S(1)}, u32[]{:S(2)}, u32[]{:S(2)}) %collective-permute-start.5) | collective-permute-done | bytes 532512 | tf_op jit(solution)/shard_map/ppermute | solution.py:67
  89.9 9.4 %collective-permute-done.6 = f32[2048,65]{0,1:T(8,128)S(1)} collective-permute-done((f32[2048,65]{0,1:T(8,128)S(1)}, f32[2048,65]{0,1:T(8,128)S(1)}, u32[]{:S(2)}, u32[]{:S(2)}) %collective-permute-start.6) | collective-permute-done | bytes 532512 | tf_op jit(solution)/shard_map/ppermute | solution.py:67
  101.4 9.1 %collective-permute-done.7 = f32[2048,65]{0,1:T(8,128)S(1)} collective-permute-done((f32[2048,65]{0,1:T(8,128)S(1)}, f32[2048,65]{0,1:T(8,128)S(1)}, u32[]{:S(2)}, u32[]{:S(2)}) %collective-permute-start.7) | collective-permute-done | bytes 532512 | tf_op jit(solution)/shard_map/ppermute | solution.py:70
  111.1 10.9 %fusion.21 = f32[2048,64]{0,1:T(8,128)S(1)} fusion(bf16[2048,4096]{1,0:T(8,128)(2,1)} %bitcast.50, bf16[4096,64]{0,1:T(8,128)(2,1)S(1)} %get-tuple-element.77), kind=kOutput, calls=%fused_computation.76 | convolution fusion | flops 1073741824 | bytes 17825792 | tf_op jit(solution)/shard_map/dot_general | solution.py:118
  122.2 6.1 %collective-permute-start.8 = (f32[1024,65]{0,1:T(8,128)S(1)}, f32[1024,65]{0,1:T(8,128)S(1)}, u32[]{:S(2)}, u32[]{:S(2)}) collective-permute-start(f32[1024,65]{0,1:T(8,128)S(1)} %slice_select_fusion.1), channel_id=1, source_target_pairs={{0,1},{1,0},{2,3},{3,2},{4,5},{5,4},{6,7},{7,6},{8,9},{9,8},{10,11... | collective-permute-start | bytes 798728 | tf_op jit(solution)/shard_map/ppermute | solution.py:65
  130.8 7.0 %collective-permute-done.9 = f32[1024,65]{0,1:T(8,128)S(1)} collective-permute-done((f32[1024,65]{0,1:T(8,128)S(1)}, f32[1024,65]{0,1:T(8,128)S(1)}, u32[]{:S(2)}, u32[]{:S(2)}) %collective-permute-start.9) | collective-permute-done | bytes 266272 | tf_op jit(solution)/shard_map/ppermute | solution.py:67
  137.9 7.3 %collective-permute-done.10 = f32[1024,65]{0,1:T(8,128)S(1)} collective-permute-done((f32[1024,65]{0,1:T(8,128)S(1)}, f32[1024,65]{0,1:T(8,128)S(1)}, u32[]{:S(2)}, u32[]{:S(2)}) %collective-permute-start.10) | collective-permute-done | bytes 266272 | tf_op jit(solution)/shard_map/ppermute | solution.py:67
  147.8 5.3 %collective-permute-done.11 = f32[1024,65]{0,1:T(8,128)S(1)} collective-permute-done((f32[1024,65]{0,1:T(8,128)S(1)}, f32[1024,65]{0,1:T(8,128)S(1)}, u32[]{:S(2)}, u32[]{:S(2)}) %collective-permute-start.11) | collective-permute-done | bytes 266272 | tf_op jit(solution)/shard_map/ppermute | solution.py:67
  157.5 9.1 %multiply_reduce_fusion.4 = (f32[64]{0:T(128)S(1)}, f32[64]{0:T(128)S(1)}, f32[4096,64]{0,1:T(8,128)S(1)}) fusion(f32[64]{0:T(128)S(1)} %copy-done.3, f32[4096]{0:T(1024)S(1)} %bitcast.60, f32[4096,65]{0,1:T(8,128)S(1)} %maximum_select_fusion, bf16[2048,64]{0,1:T(8,128)(2,1)S(1)} %slice.189, bf16[2048,4096]{1,0:T(8,128)(2,1)} %bitcast.51), kind=kOutput, calls=%fused_computation.36 | convolution fusion | flops 1075576832 | bytes 19153664 | tf_op jit(solution)/shard_map/dot_general | solution.py:126
  168.7 13.9 %collective-permute-done.13 = f32[2048,65]{0,1:T(8,128)S(1)} collective-permute-done((f32[2048,65]{0,1:T(8,128)S(1)}, f32[2048,65]{0,1:T(8,128)S(1)}, u32[]{:S(2)}, u32[]{:S(2)}) %collective-permute-start.13) | collective-permute-done | bytes 532512 | tf_op jit(solution)/shard_map/ppermute | solution.py:65
  182.8 13.6 %collective-permute-done.14 = f32[2048,65]{0,1:T(8,128)S(1)} collective-permute-done((f32[2048,65]{0,1:T(8,128)S(1)}, f32[2048,65]{0,1:T(8,128)S(1)}, u32[]{:S(2)}, u32[]{:S(2)}) %collective-permute-start.14) | collective-permute-done | bytes 532512 | tf_op jit(solution)/shard_map/ppermute | solution.py:67
  199.3 11.6 %collective-permute-done.15 = f32[2048,65]{0,1:T(8,128)S(1)} collective-permute-done((f32[2048,65]{0,1:T(8,128)S(1)}, f32[2048,65]{0,1:T(8,128)S(1)}, u32[]{:S(2)}, u32[]{:S(2)}) %collective-permute-start.15) | collective-permute-done | bytes 532512 | tf_op jit(solution)/shard_map/ppermute | solution.py:67
  212.8 11.3 %collective-permute-done.16 = f32[2048,65]{0,1:T(8,128)S(1)} collective-permute-done((f32[2048,65]{0,1:T(8,128)S(1)}, f32[2048,65]{0,1:T(8,128)S(1)}, u32[]{:S(2)}, u32[]{:S(2)}) %collective-permute-start.16) | collective-permute-done | bytes 532512 | tf_op jit(solution)/shard_map/ppermute | solution.py:70
  252.1 5.2 %fusion.22 = f32[2048,64]{0,1:T(8,128)S(1)} fusion(bf16[2048,4096]{1,0:T(8,128)(2,1)S(1)} %bitcast.54, bf16[4096,64]{0,1:T(8,128)(2,1)S(1)} %get-tuple-element.71), kind=kOutput, calls=%fused_computation.77 | convolution fusion | flops 1073741824 | bytes 17825792 | tf_op jit(solution)/shard_map/dot_general | solution.py:118
  263.7 6.3 %collective-permute-done.26 = f32[1024,64]{0,1:T(8,128)S(1)} collective-permute-done((f32[1024,64]{0,1:T(8,128)S(1)}, f32[1024,64]{0,1:T(8,128)S(1)}, u32[]{:S(2)}, u32[]{:S(2)}) %collective-permute-start.26) | collective-permute-done | bytes 262176 | tf_op jit(solution)/shard_map/ppermute | solution.py:67
  270.1 6.6 %collective-permute-done.27 = f32[1024,64]{0,1:T(8,128)S(1)} collective-permute-done((f32[1024,64]{0,1:T(8,128)S(1)}, f32[1024,64]{0,1:T(8,128)S(1)}, u32[]{:S(2)}, u32[]{:S(2)}) %collective-permute-start.27) | collective-permute-done | bytes 262176 | tf_op jit(solution)/shard_map/ppermute | solution.py:67
  279.3 4.6 %collective-permute-done.28 = f32[1024,64]{0,1:T(8,128)S(1)} collective-permute-done((f32[1024,64]{0,1:T(8,128)S(1)}, f32[1024,64]{0,1:T(8,128)S(1)}, u32[]{:S(2)}, u32[]{:S(2)}) %collective-permute-start.28) | collective-permute-done | bytes 262176 | tf_op jit(solution)/shard_map/ppermute | solution.py:67
  314.9 5.2 %fusion.23 = f32[2048,64]{0,1:T(8,128)S(1)} fusion(bf16[2048,4096]{1,0:T(8,128)(2,1)S(1)} %bitcast.56, bf16[4096,64]{0,1:T(8,128)(2,1)S(1)} %add_convert_fusion), kind=kOutput, calls=%fused_computation.78 | convolution fusion | flops 1073741824 | bytes 17825792 | tf_op jit(solution)/shard_map/dot_general | solution.py:153
  326.5 6.3 %collective-permute-done.38 = f32[1024,64]{0,1:T(8,128)S(1)} collective-permute-done((f32[1024,64]{0,1:T(8,128)S(1)}, f32[1024,64]{0,1:T(8,128)S(1)}, u32[]{:S(2)}, u32[]{:S(2)}) %collective-permute-start.38) | collective-permute-done | bytes 262176 | tf_op jit(solution)/shard_map/ppermute | solution.py:67
  332.9 6.6 %collective-permute-done.39 = f32[1024,64]{0,1:T(8,128)S(1)} collective-permute-done((f32[1024,64]{0,1:T(8,128)S(1)}, f32[1024,64]{0,1:T(8,128)S(1)}, u32[]{:S(2)}, u32[]{:S(2)}) %collective-permute-start.39) | collective-permute-done | bytes 262176 | tf_op jit(solution)/shard_map/ppermute | solution.py:67
  (164 shorter events, 156.2 us)
Async XLA Ops:
  3.4 4.8 %collective-permute-start.1 = (bf16[32,2048]{1,0:T(8,128)(2,1)S(1)}, bf16[32,2048]{1,0:T(8,128)(2,1)S(1)}, u32[]{:S(2)}, u32[]{:S(2)}) collective-permute-start(bf16[32,2048]{1,0:T(8,128)(2,1)S(1)} %maximum_select_fusion.8), channel_id=1, source_target_pairs={{0,2},{1,3},{2,0},{3,1},{4,6},{5,7},{6,4},{7,5},{8,10},{9,11},{10,... | collective-permute-start | bytes 393224 | tf_op jit(solution)/shard_map/ppermute | solution.py:80
  8.3 6.7 %collective-permute-start.2 = (bf16[64,2048]{1,0:T(8,128)(2,1)S(1)}, bf16[64,2048]{1,0:T(8,128)(2,1)S(1)}, u32[]{:S(2)}, u32[]{:S(2)}) collective-permute-start(bf16[64,2048]{1,0:T(8,128)(2,1)S(1)} %maximum_select_fusion.7), channel_id=1, source_target_pairs={{0,4},{1,5},{2,6},{3,7},{4,0},{5,1},{6,2},{7,3},{8,12},{9,13},{10,... | collective-permute-start | bytes 786440 | tf_op jit(solution)/shard_map/ppermute | solution.py:80
  15.1 13.1 %collective-permute-start.3 = (bf16[128,2048]{1,0:T(8,128)(2,1)S(1)}, bf16[128,2048]{1,0:T(8,128)(2,1)S(1)}, u32[]{:S(2)}, u32[]{:S(2)}) collective-permute-start(bf16[128,2048]{1,0:T(8,128)(2,1)S(1)} %maximum_select_fusion.4), channel_id=1, source_target_pairs={{0,12},{1,13},{2,14},{3,15},{4,8},{5,9},{6,10},{7,11},{8,4},{9,5},... | collective-permute-start | bytes 1572872 | tf_op jit(solution)/shard_map/ppermute | solution.py:80
  60.8 14.6 %collective-permute-start.4 = (f32[2048,65]{0,1:T(8,128)S(1)}, f32[2048,65]{0,1:T(8,128)S(1)}, u32[]{:S(2)}, u32[]{:S(2)}) collective-permute-start(f32[2048,65]{0,1:T(8,128)S(1)} %broadcast_select_fusion), channel_id=1, source_target_pairs={{0,48},{16,32},{32,16},{48,0},{64,112},{80,96},{96,80},{112,64},{1... | collective-permute-start | bytes 1597448 | tf_op jit(solution)/shard_map/ppermute | solution.py:65
  75.5 11.5 %collective-permute-start.5 = (f32[2048,65]{0,1:T(8,128)S(1)}, f32[2048,65]{0,1:T(8,128)S(1)}, u32[]{:S(2)}, u32[]{:S(2)}) collective-permute-start(f32[2048,65]{0,1:T(8,128)S(1)} %select_add_fusion.1), channel_id=1, source_target_pairs={{0,16},{16,0},{32,48},{48,32},{64,80},{80,64},{96,112},{112,96},{1... | collective-permute-start | bytes 1597448 | tf_op jit(solution)/shard_map/ppermute | solution.py:67
  87.1 12.2 %collective-permute-start.6 = (f32[2048,65]{0,1:T(8,128)S(1)}, f32[2048,65]{0,1:T(8,128)S(1)}, u32[]{:S(2)}, u32[]{:S(2)}) collective-permute-start(f32[2048,65]{0,1:T(8,128)S(1)} %add.202), channel_id=1, source_target_pairs={{0,64},{16,80},{32,96},{48,112},{64,0},{80,16},{96,32},{112,48},{1... | collective-permute-start | bytes 1597448 | tf_op jit(solution)/shard_map/ppermute | solution.py:67
  99.3 11.2 %collective-permute-start.7 = (f32[2048,65]{0,1:T(8,128)S(1)}, f32[2048,65]{0,1:T(8,128)S(1)}, u32[]{:S(2)}, u32[]{:S(2)}) collective-permute-start(f32[2048,65]{0,1:T(8,128)S(1)} %add.203), channel_id=1, source_target_pairs={{0,48},{16,32},{32,16},{48,0},{64,112},{80,96},{96,80},{112,64},{1... | collective-permute-start | bytes 1597448 | tf_op jit(solution)/shard_map/ppermute | solution.py:70
  122.2 7.3 %collective-permute-start.8 = (f32[1024,65]{0,1:T(8,128)S(1)}, f32[1024,65]{0,1:T(8,128)S(1)}, u32[]{:S(2)}, u32[]{:S(2)}) collective-permute-start(f32[1024,65]{0,1:T(8,128)S(1)} %slice_select_fusion.1), channel_id=1, source_target_pairs={{0,1},{1,0},{2,3},{3,2},{4,5},{5,4},{6,7},{7,6},{8,9},{9,8},{10,11... | collective-permute-start | bytes 798728 | tf_op jit(solution)/shard_map/ppermute | solution.py:65
  129.5 8.3 %collective-permute-start.9 = (f32[1024,65]{0,1:T(8,128)S(1)}, f32[1024,65]{0,1:T(8,128)S(1)}, u32[]{:S(2)}, u32[]{:S(2)}) collective-permute-start(f32[1024,65]{0,1:T(8,128)S(1)} %select_add_fusion.2), channel_id=1, source_target_pairs={{0,2},{1,3},{2,0},{3,1},{4,6},{5,7},{6,4},{7,5},{8,10},{9,11},{10,... | collective-permute-start | bytes 798728 | tf_op jit(solution)/shard_map/ppermute | solution.py:67
  137.8 7.4 %collective-permute-start.10 = (f32[1024,65]{0,1:T(8,128)S(1)}, f32[1024,65]{0,1:T(8,128)S(1)}, u32[]{:S(2)}, u32[]{:S(2)}) collective-permute-start(f32[1024,65]{0,1:T(8,128)S(1)} %add.209), channel_id=1, source_target_pairs={{0,4},{1,5},{2,6},{3,7},{4,0},{5,1},{6,2},{7,3},{8,12},{9,13},{10,... | collective-permute-start | bytes 798728 | tf_op jit(solution)/shard_map/ppermute | solution.py:67
  145.3 7.8 %collective-permute-start.11 = (f32[1024,65]{0,1:T(8,128)S(1)}, f32[1024,65]{0,1:T(8,128)S(1)}, u32[]{:S(2)}, u32[]{:S(2)}) collective-permute-start(f32[1024,65]{0,1:T(8,128)S(1)} %add.210), channel_id=1, source_target_pairs={{0,12},{1,13},{2,14},{3,15},{4,8},{5,9},{6,10},{7,11},{8,4},{9,5},... | collective-permute-start | bytes 798728 | tf_op jit(solution)/shard_map/ppermute | solution.py:67
  166.8 15.8 %collective-permute-start.13 = (f32[2048,65]{0,1:T(8,128)S(1)}, f32[2048,65]{0,1:T(8,128)S(1)}, u32[]{:S(2)}, u32[]{:S(2)}) collective-permute-start(f32[2048,65]{0,1:T(8,128)S(1)} %slice_select_fusion), channel_id=1, source_target_pairs={{0,48},{16,32},{32,16},{48,0},{64,112},{80,96},{96,80},{112,64},{1... | collective-permute-start | bytes 1597448 | tf_op jit(solution)/shard_map/ppermute | solution.py:65
  182.7 13.7 %collective-permute-start.14 = (f32[2048,65]{0,1:T(8,128)S(1)}, f32[2048,65]{0,1:T(8,128)S(1)}, u32[]{:S(2)}, u32[]{:S(2)}) collective-permute-start(f32[2048,65]{0,1:T(8,128)S(1)} %select_add_fusion), channel_id=1, source_target_pairs={{0,16},{16,0},{32,48},{48,32},{64,80},{80,64},{96,112},{112,96},{1... | collective-permute-start | bytes 1597448 | tf_op jit(solution)/shard_map/ppermute | solution.py:67
  196.5 14.4 %collective-permute-start.15 = (f32[2048,65]{0,1:T(8,128)S(1)}, f32[2048,65]{0,1:T(8,128)S(1)}, u32[]{:S(2)}, u32[]{:S(2)}) collective-permute-start(f32[2048,65]{0,1:T(8,128)S(1)} %add.214), channel_id=1, source_target_pairs={{0,64},{16,80},{32,96},{48,112},{64,0},{80,16},{96,32},{112,48},{1... | collective-permute-start | bytes 1597448 | tf_op jit(solution)/shard_map/ppermute | solution.py:67
  210.9 13.2 %collective-permute-start.16 = (f32[2048,65]{0,1:T(8,128)S(1)}, f32[2048,65]{0,1:T(8,128)S(1)}, u32[]{:S(2)}, u32[]{:S(2)}) collective-permute-start(f32[2048,65]{0,1:T(8,128)S(1)} %add.215), channel_id=1, source_target_pairs={{0,48},{16,32},{32,16},{48,0},{64,112},{80,96},{96,80},{112,64},{1... | collective-permute-start | bytes 1597448 | tf_op jit(solution)/shard_map/ppermute | solution.py:70
  224.3 4.7 %collective-permute-start.17 = (f32[64]{0:T(128)S(1)}, f32[64]{0:T(128)S(1)}, u32[]{:S(2)}, u32[]{:S(2)}) collective-permute-start(f32[64]{0:T(128)S(1)} %slice_bitcast_fusion), channel_id=1, source_target_pairs={{0,1},{1,0},{2,3},{3,2},{4,5},{5,4},{6,7},{7,6},{8,9},{9,8},{10,11... | collective-permute-start | bytes 776 | tf_op jit(solution)/shard_map/ppermute | solution.py:50
  257.3 5.0 %collective-permute-start.25 = (f32[1024,64]{0,1:T(8,128)S(1)}, f32[1024,64]{0,1:T(8,128)S(1)}, u32[]{:S(2)}, u32[]{:S(2)}) collective-permute-start(f32[1024,64]{0,1:T(8,128)S(1)} %slice_select_fusion.3), channel_id=1, source_target_pairs={{0,1},{1,0},{2,3},{3,2},{4,5},{5,4},{6,7},{7,6},{8,9},{9,8},{10,11... | collective-permute-start | bytes 786440 | tf_op jit(solution)/shard_map/ppermute | solution.py:65
  262.4 7.6 %collective-permute-start.26 = (f32[1024,64]{0,1:T(8,128)S(1)}, f32[1024,64]{0,1:T(8,128)S(1)}, u32[]{:S(2)}, u32[]{:S(2)}) collective-permute-start(f32[1024,64]{0,1:T(8,128)S(1)} %select_add_fusion.4), channel_id=1, source_target_pairs={{0,2},{1,3},{2,0},{3,1},{4,6},{5,7},{6,4},{7,5},{8,10},{9,11},{10,... | collective-permute-start | bytes 786440 | tf_op jit(solution)/shard_map/ppermute | solution.py:67
  270.0 6.7 %collective-permute-start.27 = (f32[1024,64]{0,1:T(8,128)S(1)}, f32[1024,64]{0,1:T(8,128)S(1)}, u32[]{:S(2)}, u32[]{:S(2)}) collective-permute-start(f32[1024,64]{0,1:T(8,128)S(1)} %add.227), channel_id=1, source_target_pairs={{0,4},{1,5},{2,6},{3,7},{4,0},{5,1},{6,2},{7,3},{8,12},{9,13},{10,... | collective-permute-start | bytes 786440 | tf_op jit(solution)/shard_map/ppermute | solution.py:67
  276.8 7.1 %collective-permute-start.28 = (f32[1024,64]{0,1:T(8,128)S(1)}, f32[1024,64]{0,1:T(8,128)S(1)}, u32[]{:S(2)}, u32[]{:S(2)}) collective-permute-start(f32[1024,64]{0,1:T(8,128)S(1)} %add.228), channel_id=1, source_target_pairs={{0,12},{1,13},{2,14},{3,15},{4,8},{5,9},{6,10},{7,11},{8,4},{9,5},... | collective-permute-start | bytes 786440 | tf_op jit(solution)/shard_map/ppermute | solution.py:67
  320.1 5.0 %collective-permute-start.37 = (f32[1024,64]{0,1:T(8,128)S(1)}, f32[1024,64]{0,1:T(8,128)S(1)}, u32[]{:S(2)}, u32[]{:S(2)}) collective-permute-start(f32[1024,64]{0,1:T(8,128)S(1)} %slice_select_fusion.2), channel_id=1, source_target_pairs={{0,1},{1,0},{2,3},{3,2},{4,5},{5,4},{6,7},{7,6},{8,9},{9,8},{10,11... | collective-permute-start | bytes 786440 | tf_op jit(solution)/shard_map/ppermute | solution.py:65
  325.2 7.6 %collective-permute-start.38 = (f32[1024,64]{0,1:T(8,128)S(1)}, f32[1024,64]{0,1:T(8,128)S(1)}, u32[]{:S(2)}, u32[]{:S(2)}) collective-permute-start(f32[1024,64]{0,1:T(8,128)S(1)} %select_add_fusion.3), channel_id=1, source_target_pairs={{0,2},{1,3},{2,0},{3,1},{4,6},{5,7},{6,4},{7,5},{8,10},{9,11},{10,... | collective-permute-start | bytes 786440 | tf_op jit(solution)/shard_map/ppermute | solution.py:67
  332.8 6.7 %collective-permute-start.39 = (f32[1024,64]{0,1:T(8,128)S(1)}, f32[1024,64]{0,1:T(8,128)S(1)}, u32[]{:S(2)}, u32[]{:S(2)}) collective-permute-start(f32[1024,64]{0,1:T(8,128)S(1)} %add.240), channel_id=1, source_target_pairs={{0,4},{1,5},{2,6},{3,7},{4,0},{5,1},{6,2},{7,3},{8,12},{9,13},{10,... | collective-permute-start | bytes 786440 | tf_op jit(solution)/shard_map/ppermute | solution.py:67
  339.6 7.1 %collective-permute-start.40 = (f32[1024,64]{0,1:T(8,128)S(1)}, f32[1024,64]{0,1:T(8,128)S(1)}, u32[]{:S(2)}, u32[]{:S(2)}) collective-permute-start(f32[1024,64]{0,1:T(8,128)S(1)} %add.241), channel_id=1, source_target_pairs={{0,12},{1,13},{2,14},{3,15},{4,8},{5,9},{6,10},{7,11},{8,4},{9,5},... | collective-permute-start | bytes 786440 | tf_op jit(solution)/shard_map/ppermute | solution.py:67
  (26 other events, 507.4 us)
